TPU v7x, 256 devices: a whole 4x4x8 slice. The times are simulated.
256 devices in a mesh: pb: 8 (over y, core), kv: 32 (over z, x).
Axes of the slice: x: 4, y: 4, z: 8, core: 2. Of those that a mesh axis runs over, the one named last changes fastest.
Arguments:
- queries: bfloat16 [65536, 4096], P(('pb', 'kv')), may hold values from -6 to 6
- keys: bfloat16 [8192, 4096], P(('pb', 'kv')), may hold values from -6 to 6
- values: bfloat16 [8192, 4096], P(('pb', 'kv')), may hold values from -6 to 6
- key_lists: int32 [512, 8], P('pb'), may hold values from 0 to 63, as said below
- counts: int32 [512], P('pb'), may hold values from 1 to 8, as said below
Outputs:
- attended: bfloat16 [65536, 4096], P(('pb', 'kv'))
Inputs may be any that keep to these rules, and one draw needn't show every extreme that they name: For every query block the first counts entries of its row of key_lists name different key blocks; entries past counts are valid block numbers that do not take part. `counts`: some query block uses all 8 entries of its list.
All inputs are finite; a program needn't handle non-finite values.
Results may differ from a plain program's by a relative error of at most 0.011.
Values may be sent and summed in bfloat16 or wider, within the bound.
No kernel may reach another device: no remote copies, remote signals or barrier semaphores. Data moves between devices by JAX's collectives and lax.ppermute only.
A program may use at most 64 MiB of HBM per device.

v0:
```python
import functools

import jax
import jax.numpy as jnp
from jax import lax
from jax.experimental import pallas as pl
from jax.experimental.pallas import tpu as pltpu
from jax.sharding import PartitionSpec as P

HEADS = 32
HD = 128
BLK = 128
MOST = 8


def attend_kernel(lists_ref, counts_ref, q_ref, kv_ref, o_ref, kc_ref, vc_ref, *, per_step, scaling):
    step = pl.program_id(1)

    def one(i, carry):
        qb = step * per_step + i
        cnt = counts_ref[qb]
        q = q_ref[i]
        for s in range(MOST):
            kb = lists_ref[qb * MOST + s]
            start = pl.multiple_of(kb * BLK, BLK)
            kc_ref[pl.ds(s * BLK, BLK), :] = kv_ref[pl.ds(start, BLK), pl.ds(0, HD)]
            vc_ref[pl.ds(s * BLK, BLK), :] = kv_ref[pl.ds(start, BLK), pl.ds(HD, HD)]
        sc = lax.dot_general(q, kc_ref[...], (((1,), (1,)), ((), ())),
                             preferred_element_type=jnp.float32) * scaling
        slot = lax.broadcasted_iota(jnp.int32, sc.shape, 1) // BLK
        sc = jnp.where(slot < cnt, sc, -jnp.inf)
        m = jnp.max(sc, axis=-1, keepdims=True)
        p = jnp.exp(sc - m)
        l = jnp.sum(p, axis=-1, keepdims=True)
        w = (p / l).astype(jnp.bfloat16)
        out = jnp.dot(w, vc_ref[...], preferred_element_type=jnp.float32)
        o_ref[i] = out.astype(o_ref.dtype)
        return carry

    lax.fori_loop(0, per_step, one, 0, unroll=2)


def attend(q_blocks, kv_rows, lists, counts, head_local):
    blocks = q_blocks.shape[0]
    per_step = 8 if blocks % 8 == 0 else 2
    nk = kv_rows.shape[0]
    kernel = functools.partial(attend_kernel, per_step=per_step, scaling=HD ** (-0.5))
    flops = blocks * head_local * MOST * 4 * BLK * BLK * HD
    grid_spec = pltpu.PrefetchScalarGridSpec(
        num_scalar_prefetch=2,
        grid=(head_local, blocks // per_step),
        in_specs=[
            pl.BlockSpec((per_step, BLK, HD), lambda h, b, *_: (b, 0, h)),
            pl.BlockSpec((nk, 2 * HD), lambda h, b, *_: (0, h)),
        ],
        out_specs=pl.BlockSpec((per_step, BLK, HD), lambda h, b, *_: (b, 0, h)),
        scratch_shapes=[
            pltpu.VMEM((MOST * BLK, HD), jnp.bfloat16),
            pltpu.VMEM((MOST * BLK, HD), jnp.bfloat16),
        ],
    )
    return pl.pallas_call(
        kernel,
        grid_spec=grid_spec,
        out_shape=jax.ShapeDtypeStruct(q_blocks.shape, jnp.bfloat16),
        compiler_params=pltpu.CompilerParams(dimension_semantics=("arbitrary", "arbitrary")),
        cost_estimate=pl.CostEstimate(
            flops=flops,
            transcendentals=blocks * head_local * BLK * MOST * BLK,
            bytes_accessed=kv_rows.size * 2 + q_blocks.size * 4,
        ),
    )(lists.reshape(-1), counts, q_blocks, kv_rows)


def per_device(queries, keys, values, key_lists, counts):
    kv_count = lax.axis_size("kv")
    head_local = HEADS // kv_count
    tokens = keys.shape[0]
    stacked = jnp.stack(
        [keys.reshape(tokens, HEADS, HD), values.reshape(tokens, HEADS, HD)], axis=2
    )
    kv_split = lax.all_to_all(stacked, "kv", split_axis=1, concat_axis=0, tiled=True)
    kv_whole = lax.all_gather(kv_split, "pb", axis=0, tiled=True)
    kv_rows = kv_whole.reshape(kv_whole.shape[0], head_local * 2 * HD)

    query_blocks = queries.reshape(-1, BLK, queries.shape[1])
    exchanged = lax.all_to_all(query_blocks, "kv", split_axis=2, concat_axis=0, tiled=True)
    produced = attend(exchanged, kv_rows, key_lists, counts, head_local)
    result = lax.all_to_all(produced, "kv", split_axis=0, concat_axis=2, tiled=True)
    return result.reshape(queries.shape)


def solution(mesh):
    return jax.shard_map(
        per_device,
        mesh=mesh,
        in_specs=(
            P(("pb", "kv"), None),
            P(("pb", "kv"), None),
            P(("pb", "kv"), None),
            P("pb", None),
            P("pb"),
        ),
        out_specs=P(("pb", "kv"), None),
        check_vma=False,
    )
```

profile of v0, /device:TPU:1, one launch (start us, length us, event | category | flops | bytes accessed | tf_op | source)
XLA Modules:
  0.0 211.7 jit_solution(2598691766614673907)
XLA Ops:
  6.5 0.0 all-gather.2.cloned.1.call-start
  6.5 1.0 copy.30
  7.5 1.0 copy.31
  8.5 0.1 pad_maximum_fusion
  8.6 0.2 copy.26
  8.8 0.0 copy-start
  8.8 28.1 %all_to_all.51 = bf16[32,32,2,128]{3,0,2,1:T(8,128)(2,1)S(1)} all-to-all(bf16[32,32,2,128]{3,0,2,1:T(8,128)(2,1)S(1)} %copy.26), channel_id=1, replica_groups=mesh['pb'=8,'kv'=32] {'kv'}, dimensions={1} | all-to-all | bytes 1048576 | tf_op jit(solution)/shard_map/all_to_all | solution.py:82
  36.9 1.3 copy.28
  38.3 0.0 all-gather.2.cloned.1.call-update
  38.3 0.0 copy-done
  38.3 3.8 %copy.23 = bf16[2,128,4096]{1,0,2:T(2,128)(2,1)} copy(bf16[2,128,4096]{2,1,0:T(8,128)(2,1)S(1)} %bitcast.36) | data formatting | bytes 4194304 | tf_op jit(solution)/shard_map/reshape | solution.py:86
  42.1 0.0 copy-start.1
  42.1 5.3 %all-to-all-start = ((bf16[2,128,4096]{1,0,2:T(2,128)(2,1)}), bf16[2,128,4096]{1,0,2:T(2,128)(2,1)S(1)}, u32[]{:S(2)}, u32[]{:S(2)}) async-start(bf16[2,128,4096]{1,0,2:T(2,128)(2,1)} %copy.23), calls=%async_computation | async-start | bytes 4194304 | tf_op jit(solution)/shard_map/all_to_all | solution.py:87
  47.4 0.0 copy-done.1
  47.4 0.1 copy.22
  47.5 0.6 reshape.13.lists_ref
  48.2 46.9 %all-to-all-done = bf16[2,128,4096]{1,0,2:T(2,128)(2,1)S(1)} async-done(((bf16[2,128,4096]{1,0,2:T(2,128)(2,1)}), bf16[2,128,4096]{1,0,2:T(2,128)(2,1)S(1)}, u32[]{:S(2)}, u32[]{:S(2)}) %all-to-all-start) | async-done | bytes 2097184 | tf_op jit(solution)/shard_map/all_to_all | solution.py:87
  95.1 1.6 copy.24
  96.6 4.1 %copy.25 = bf16[32,2,128,128]{3,2,1,0:T(8,128)(2,1)} copy(bf16[32,2,128,128]{2,3,0,1:T(8,128)(2,1)} %bitcast.31) | data formatting | bytes 4194304 | tf_op jit(solution)/shard_map/all_to_all | solution.py:87
  100.7 0.0 all-gather.2.cloned.1.call-done
  100.7 4.7 %copy.36 = bf16[1024,8,2,128]{3,1,2,0:T(8,128)(2,1)} copy(bf16[1024,8,2,128]{3,2,1,0:T(2,128)(2,1)} %bitcast.34) | data formatting | bytes 8388608
  105.4 41.9 %shard_map.55 = bf16[64,128,128]{2,1,0:T(8,128)(2,1)} custom-call(s32[512]{0:T(512)} %reshape.13.lists_ref, s32[64]{0:T(128)} %counts_ref.1, bf16[64,128,128]{2,1,0:T(8,128)(2,1)} %bitcast.37, bf16[8192,256]{1,0:T(8,128)(2,1)} %bitcast.35), custom_call_target="tpu_custom_call" | custom-call | flops 4294967296 | bytes 8388608 | tf_op jit(solution)/shard_map/pallas_call | solution.py:62
  147.3 53.8 %all_to_all.52 = bf16[64,128,128]{2,1,0:T(8,128)(2,1)S(1)} all-to-all(bf16[64,128,128]{2,1,0:T(8,128)(2,1)} %shard_map.55), channel_id=1, replica_groups=mesh['pb'=8,'kv'=32] {'kv'}, dimensions={0} | all-to-all | bytes 4194304 | tf_op jit(solution)/shard_map/all_to_all | solution.py:89
  201.2 1.4 copy.29
  202.5 2.3 %copy.37 = bf16[32,8,32,128]{3,1,2,0:T(8,128)(2,1)} copy(bf16[32,8,32,128]{3,2,1,0:T(8,128)(2,1)S(1)} %bitcast.33) | data formatting | bytes 4194304
  (1 shorter events, 0.0 us)
Async XLA Ops:
  6.5 94.2 %all-gather.2.cloned.1.call-start = ((), (), s32[]{:S(2)}) async-start(), calls=%async_computation.3 | async-start | bytes 4718592 | tf_op jit(solution)/shard_map/all_gather | solution.py:83
  8.8 29.5 %copy-start = (bf16[256,4096]{1,0:T(8,128)(2,1)S(1)}, bf16[256,4096]{1,0:T(8,128)(2,1)}, u32[]{:S(2)}) copy-start(bf16[256,4096]{1,0:T(8,128)(2,1)} %param.5) | copy-start | bytes 6291460
  42.1 5.4 %copy-start.1 = (s32[64,8]{0,1:T(8,128)S(1)}, s32[64,8]{0,1:T(8,128)}, u32[]{:S(2)}) copy-start(s32[64,8]{0,1:T(8,128)} %param.8) | copy-start | bytes 6148
  42.1 53.0 %all-to-all-start = ((bf16[2,128,4096]{1,0,2:T(2,128)(2,1)}), bf16[2,128,4096]{1,0,2:T(2,128)(2,1)S(1)}, u32[]{:S(2)}, u32[]{:S(2)}) async-start(bf16[2,128,4096]{1,0,2:T(2,128)(2,1)} %copy.23), calls=%async_computation | async-start | bytes 4194304 | tf_op jit(solution)/shard_map/all_to_all | solution.py:87
Sparse Core Ops, SparseCore 0:
  38.4 33.1 all-gather.1
where the time goes:
time: 216 us; the launch traced here: 212 us
  blocking collectives  81.9 us (38%)
  waiting for transfers between devices  46.9 us (22%)
  Pallas kernels  41.9 us (19%)
  local copies, waits for them, and re-layouts  22.1 us (10%)
  between operations  13.5 us (6%)
  starting transfers between devices  5.34 us (2%)
    all_to_all x1, blocking collectives, per_device(): lax.all_to_all(produced, 'kv', split_axis=0, concat_axis=2, tiled=True)  53.8 us
    all_to_all x1, waiting for transfers between devices, per_device(): lax.all_to_all(query_blocks, 'kv', split_axis=2, concat_axis=0, tiled=True)  46.9 us
    pallas_call x1, Pallas kernels, attend(): pl.pallas_call(kernel, grid_spec=grid_spec, out_shape=jax.ShapeDtypeStruc...  41.9 us
    all_to_all x1, blocking collectives, per_device(): lax.all_to_all(stacked, 'kv', split_axis=1, concat_axis=0, tiled=True)  28.1 us
    unnamed x9, local copies, waits for them, and re-layouts  9.08 us
    all_to_all x2, local copies, waits for them, and re-layouts, per_device(): lax.all_to_all(query_blocks, 'kv', split_axis=2, concat_axis=0, tiled=True)  5.65 us
    all_to_all x1, starting transfers between devices, per_device(): lax.all_to_all(query_blocks, 'kv', split_axis=2, concat_axis=0, tiled=True)  5.34 us
  transfers between devices with their start and end apart: 2, of which 1 were waited for; matrix products, arithmetic and copies ran while one was open for 5% of the time, Pallas kernels for 0%

commit v1 on v0

--- a/solution.py
+++ b/solution.py
@@ -72,35 +72,52 @@
     )(lists.reshape(-1), counts, q_blocks, kv_rows)
 
 
-def per_device(queries, keys, values, key_lists, counts):
-    kv_count = lax.axis_size("kv")
-    head_local = HEADS // kv_count
+def per_device(queries, keys, values, key_lists, counts, *, x_count):
+    group = ("y", "core", "x")
+    pb_count = lax.axis_size("y") * lax.axis_size("core")
+    z_count = lax.axis_size("z")
+    group_count = pb_count * x_count
+    kv_count = z_count * x_count
+    head_local = HEADS // group_count
     tokens = keys.shape[0]
+    assert BLK == x_count * tokens
     stacked = jnp.stack(
         [keys.reshape(tokens, HEADS, HD), values.reshape(tokens, HEADS, HD)], axis=2
     )
-    kv_split = lax.all_to_all(stacked, "kv", split_axis=1, concat_axis=0, tiled=True)
-    kv_whole = lax.all_gather(kv_split, "pb", axis=0, tiled=True)
+    kv_split = lax.all_to_all(stacked, group, split_axis=1, concat_axis=0, tiled=True)
+    kv_whole = lax.all_gather(kv_split, "z", axis=0, tiled=True)
     kv_rows = kv_whole.reshape(kv_whole.shape[0], head_local * 2 * HD)
 
+    all_lists = lax.all_gather(key_lists, ("y", "core"), axis=0, tiled=True)
+    all_counts = lax.all_gather(counts, ("y", "core"), axis=0, tiled=True)
+    per_dev = queries.shape[0] // BLK
+    member = jnp.arange(group_count, dtype=jnp.int32)
+    first = ((member // x_count) * kv_count + member % x_count) * per_dev
+    ids = (first[:, None] + jnp.arange(per_dev, dtype=jnp.int32)[None, :]).reshape(-1)
+    ids = ids + lax.axis_index("z") * (x_count * per_dev)
+    lists = all_lists[ids]
+    lists = (lists % z_count) * pb_count + lists // z_count
+    local_counts = all_counts[ids]
+
     query_blocks = queries.reshape(-1, BLK, queries.shape[1])
-    exchanged = lax.all_to_all(query_blocks, "kv", split_axis=2, concat_axis=0, tiled=True)
-    produced = attend(exchanged, kv_rows, key_lists, counts, head_local)
-    result = lax.all_to_all(produced, "kv", split_axis=0, concat_axis=2, tiled=True)
+    exchanged = lax.all_to_all(query_blocks, group, split_axis=2, concat_axis=0, tiled=True)
+    produced = attend(exchanged, kv_rows, lists, local_counts, head_local)
+    result = lax.all_to_all(produced, group, split_axis=0, concat_axis=2, tiled=True)
     return result.reshape(queries.shape)
 
 
 def solution(mesh):
+    pb_count, kv_count = mesh.shape["pb"], mesh.shape["kv"]
+    x_count = 4
+    fine = jax.sharding.Mesh(
+        mesh.devices.reshape(pb_count // 2, 2, kv_count // x_count, x_count),
+        ("y", "core", "z", "x"),
+    )
+    rows = P(("y", "core", "z", "x"), None)
     return jax.shard_map(
-        per_device,
-        mesh=mesh,
-        in_specs=(
-            P(("pb", "kv"), None),
-            P(("pb", "kv"), None),
-            P(("pb", "kv"), None),
-            P("pb", None),
-            P("pb"),
-        ),
-        out_specs=P(("pb", "kv"), None),
+        functools.partial(per_device, x_count=x_count),
+        mesh=fine,
+        in_specs=(rows, rows, rows, P(("y", "core"), None), P(("y", "core"))),
+        out_specs=rows,
         check_vma=False,
     )

time: 216 us -> 180 us (0.83); the launches traced: 212 us -> 179 us
  waiting for transfers between devices: 46.9 us -> 0.02 us
  blocking collectives: 81.9 us -> 93.5 us
  local copies, waits for them, and re-layouts: 22.1 us -> 24.5 us
    all_to_all x1, waiting for transfers between devices: 46.9 us -> 0.01 us  [per_device(): lax.all_to_all(query_blocks, group, split_axis=2, concat_axis=0, tiled=True)]
    all_gather x0 -> x1, blocking collectives: none -> 30.1 us  [per_device(): all_lists = lax.all_gather(key_lists, ('y', 'core'), axis=0, tiled=True)]
    all_to_all x2, blocking collectives: 81.9 us -> 54.2 us  [the longest x1 34.3 us: per_device(): lax.all_to_all(produced, group, split_axis=0, concat_axis=2, tiled=True)]
    unnamed x0 -> x1, blocking collectives: none -> 9.19 us
    unnamed x9 -> x14, local copies, waits for them, and re-layouts: 9.08 us -> 9.89 us
  transfers between devices with their start and end apart: 2 -> 2, of which waited for: 1 -> 0; matrix products, arithmetic and copies ran while one was open for 5% -> 7% of each run, Pallas kernels for 0% -> 0%
where the time goes in v1:
time: 180 us; the launch traced here: 179 us
  blocking collectives  93.5 us (52%)
  Pallas kernels  41.9 us (23%)
  local copies, waits for them, and re-layouts  24.5 us (14%)
  between operations  14.2 us (8%)
  starting transfers between devices  4.48 us (2%)
    pallas_call x1, Pallas kernels, attend(): pl.pallas_call(kernel, grid_spec=grid_spec, out_shape=jax.ShapeDtypeStruc...  41.9 us
    all_to_all x1, blocking collectives, per_device(): lax.all_to_all(produced, group, split_axis=0, concat_axis=2, tiled=True)  34.3 us
    all_gather x1, blocking collectives, per_device(): all_lists = lax.all_gather(key_lists, ('y', 'core'), axis=0, tiled=True)  30.1 us
    all_to_all x1, blocking collectives, per_device(): lax.all_to_all(stacked, group, split_axis=1, concat_axis=0, tiled=True)  19.9 us
    unnamed x14, local copies, waits for them, and re-layouts  9.89 us
    unnamed x1, blocking collectives  9.19 us
    all_to_all x2, local copies, waits for them, and re-layouts, per_device(): lax.all_to_all(query_blocks, group, split_axis=2, concat_axis=0, tiled=True)  5.65 us
    all_to_all x1, starting transfers between devices, per_device(): lax.all_to_all(query_blocks, group, split_axis=2, concat_axis=0, tiled=True)  4.48 us
  transfers between devices with their start and end apart: 2, of which 0 were waited for; matrix products, arithmetic and copies ran while one was open for 7% of the time, Pallas kernels for 0%

profile of v1, /device:TPU:1, one launch (start us, length us, event | category | flops | bytes accessed | tf_op | source)
XLA Modules:
  0.0 179.4 jit_solution(11205285138930218463)
XLA Ops:
  6.5 0.0 all-gather.3.cloned.1.call-start
  6.5 1.0 copy.31
  7.5 1.0 copy.32
  8.5 0.1 pad_maximum_fusion
  8.6 0.2 copy.27
  8.8 0.0 copy-start
  8.8 19.9 %all_to_all.51 = bf16[32,32,2,128]{3,0,2,1:T(8,128)(2,1)S(1)} all-to-all(bf16[32,32,2,128]{3,0,2,1:T(8,128)(2,1)S(1)} %copy.27), channel_id=1, replica_groups=mesh['y'=4,'core'=2,'z'=8,'x'=4] {'y','core','x'}, dimensions={1} | all-to-all | bytes 1048576 | tf_op jit(solution)/shard_map/all_to_all | solution.py:87
  28.8 1.3 copy.29
  30.1 0.0 all-gather.3.cloned.1.call-update
  30.1 0.0 copy-done
  30.1 3.8 %copy.24 = bf16[2,128,4096]{1,0,2:T(2,128)(2,1)} copy(bf16[2,128,4096]{2,1,0:T(8,128)(2,1)S(1)} %bitcast.41) | data formatting | bytes 4194304 | tf_op jit(solution)/shard_map/reshape | solution.py:102
  33.9 4.5 %all-to-all-start = ((bf16[2,128,4096]{1,0,2:T(2,128)(2,1)}), bf16[2,128,4096]{1,0,2:T(2,128)(2,1)S(1)}, u32[]{:S(2)}, u32[]{:S(2)}) async-start(bf16[2,128,4096]{1,0,2:T(2,128)(2,1)} %copy.24), calls=%async_computation | async-start | bytes 4194304 | tf_op jit(solution)/shard_map/all_to_all | solution.py:103
  38.4 0.1 add_add_fusion
  38.5 0.1 add.91
  38.6 0.0 copy-done.1
  38.6 30.1 %all-gather = s32[8,64,8]{1,2,0:T(8,128)S(1)} all-gather(s32[1,64,8]{1,2,0:T(8,128)S(1)} %bitcast.49), channel_id=1, replica_groups=mesh['y'=4,'core'=2,'z'=8,'x'=4] {'y','core'}, dimensions={0}, use_global_device_ids=true | all-gather | bytes 18432 | tf_op jit(solution)/shard_map/all_gather | solution.py:91
  68.8 0.1 copy.23
  68.9 0.7 dynamic-slice
  70.2 0.2 dynamic-update-slice
  70.5 9.2 %all-reduce = s32[512]{0:T(512)S(1)} all-reduce(s32[512]{0:T(512)S(1)} %dynamic-update-slice), channel_id=1, replica_groups=mesh['y'=4,'core'=2,'z'=8,'x'=4] {'y','core'}, use_global_device_ids=true, to_apply=%add | all-reduce | flops 512 | bytes 4096
  79.7 1.4 gather_fusion.1
  81.0 0.6 gather_fusion
  81.6 0.1 gather.9
  81.7 0.6 fusion.1.lists_ref
  82.3 0.0 all-to-all-done
  82.3 1.6 copy.25
  83.9 4.1 %copy.26 = bf16[32,2,128,128]{3,2,1,0:T(8,128)(2,1)} copy(bf16[32,2,128,128]{2,3,0,1:T(8,128)(2,1)} %bitcast.36) | data formatting | bytes 4194304 | tf_op jit(solution)/shard_map/all_to_all | solution.py:103
  87.9 4.7 %copy.37 = bf16[1024,8,2,128]{3,1,2,0:T(8,128)(2,1)} copy(bf16[1024,8,2,128]{3,2,1,0:T(2,128)(2,1)} %bitcast.39) | data formatting | bytes 8388608
  92.6 41.9 %shard_map.55 = bf16[64,128,128]{2,1,0:T(8,128)(2,1)} custom-call(s32[512]{0:T(512)} %fusion.1.lists_ref, s32[64]{0:T(128)} %gather_fusion.1, bf16[64,128,128]{2,1,0:T(8,128)(2,1)} %bitcast.42, bf16[8192,256]{1,0:T(8,128)(2,1)} %bitcast.40), custom_call_target="tpu_custom_call" | custom-call | flops 4294967296 | bytes 8388608 | tf_op jit(solution)/shard_map/pallas_call | solution.py:62
  134.6 34.3 %all_to_all.52 = bf16[64,128,128]{2,1,0:T(8,128)(2,1)S(1)} all-to-all(bf16[64,128,128]{2,1,0:T(8,128)(2,1)} %shard_map.55), channel_id=1, replica_groups=mesh['y'=4,'core'=2,'z'=8,'x'=4] {'y','core','x'}, dimensions={0} | all-to-all | bytes 4194304 | tf_op jit(solution)/shard_map/all_to_all | solution.py:105
  168.9 1.4 copy.30
  170.2 2.3 %copy.38 = bf16[32,8,32,128]{3,1,2,0:T(8,128)(2,1)} copy(bf16[32,8,32,128]{3,2,1,0:T(8,128)(2,1)S(1)} %bitcast.38) | data formatting | bytes 4194304
  (11 shorter events, 0.1 us)
Async XLA Ops:
  6.5 81.4 %all-gather.3.cloned.1.call-start = ((), (), s32[]{:S(2)}) async-start(), calls=%async_computation.3 | async-start | bytes 4718592 | tf_op jit(solution)/shard_map/all_gather | solution.py:88
  8.8 21.3 %copy-start = (bf16[256,4096]{1,0:T(8,128)(2,1)S(1)}, bf16[256,4096]{1,0:T(8,128)(2,1)}, u32[]{:S(2)}) copy-start(bf16[256,4096]{1,0:T(8,128)(2,1)} %param.5) | copy-start | bytes 6291460
  33.9 4.7 %copy-start.1 = (s32[64,8]{0,1:T(8,128)S(1)}, s32[64,8]{0,1:T(8,128)}, u32[]{:S(2)}) copy-start(s32[64,8]{0,1:T(8,128)} %param.8) | copy-start | bytes 6148
  33.9 35.0 %copy-start.3 = (u32[256]{0:T(256)S(1)}, u32[256]{0:T(256)}, u32[]{:S(2)}) copy-start(u32[256]{0:T(256)} %constant.72) | copy-start | bytes 3076
  33.9 36.3 %copy-start.2 = (s32[64]{0:T(128)S(1)}, s32[64]{0:T(128)}, u32[]{:S(2)}) copy-start(s32[64]{0:T(128)} %param.9) | copy-start | bytes 772
  33.9 48.4 %all-to-all-start = ((bf16[2,128,4096]{1,0,2:T(2,128)(2,1)}), bf16[2,128,4096]{1,0,2:T(2,128)(2,1)S(1)}, u32[]{:S(2)}, u32[]{:S(2)}) async-start(bf16[2,128,4096]{1,0,2:T(2,128)(2,1)} %copy.24), calls=%async_computation | async-start | bytes 4194304 | tf_op jit(solution)/shard_map/all_to_all | solution.py:103
Sparse Core Ops, SparseCore 0:
  30.3 54.3 all-gather.2

commit v2 on v1

--- a/solution.py
+++ b/solution.py
@@ -81,23 +81,35 @@
     head_local = HEADS // group_count
     tokens = keys.shape[0]
     assert BLK == x_count * tokens
-    stacked = jnp.stack(
-        [keys.reshape(tokens, HEADS, HD), values.reshape(tokens, HEADS, HD)], axis=2
+    per_dev = queries.shape[0] // BLK
+    meta_width = per_dev * (MOST + 1)
+    assert meta_width <= 2 * HD
+    kv_index = lax.axis_index("z") * x_count + lax.axis_index("x")
+    own_lists = lax.dynamic_slice_in_dim(key_lists, kv_index * per_dev, per_dev, axis=0)
+    own_counts = lax.dynamic_slice_in_dim(counts, kv_index * per_dev, per_dev, axis=0)
+    meta = jnp.concatenate([own_lists, own_counts[:, None]], axis=1).reshape(-1)
+    meta_row = jnp.zeros((2 * HD,), jnp.bfloat16).at[:meta_width].set(meta.astype(jnp.bfloat16))
+    meta_token = jnp.broadcast_to(meta_row.reshape(1, 1, 2, HD), (1, HEADS, 2, HD))
+    stacked = jnp.concatenate(
+        [
+            jnp.stack(
+                [keys.reshape(tokens, HEADS, HD), values.reshape(tokens, HEADS, HD)], axis=2
+            ),
+            meta_token,
+        ],
+        axis=0,
     )
     kv_split = lax.all_to_all(stacked, group, split_axis=1, concat_axis=0, tiled=True)
-    kv_whole = lax.all_gather(kv_split, "z", axis=0, tiled=True)
+    kv_split = kv_split.reshape(group_count, tokens + 1, head_local, 2, HD)
+    kv_part = kv_split[:, :tokens].reshape(group_count * tokens, head_local, 2, HD)
+    kv_whole = lax.all_gather(kv_part, "z", axis=0, tiled=True)
     kv_rows = kv_whole.reshape(kv_whole.shape[0], head_local * 2 * HD)
 
-    all_lists = lax.all_gather(key_lists, ("y", "core"), axis=0, tiled=True)
-    all_counts = lax.all_gather(counts, ("y", "core"), axis=0, tiled=True)
-    per_dev = queries.shape[0] // BLK
-    member = jnp.arange(group_count, dtype=jnp.int32)
-    first = ((member // x_count) * kv_count + member % x_count) * per_dev
-    ids = (first[:, None] + jnp.arange(per_dev, dtype=jnp.int32)[None, :]).reshape(-1)
-    ids = ids + lax.axis_index("z") * (x_count * per_dev)
-    lists = all_lists[ids]
+    meta_in = kv_split[:, tokens, 0].reshape(group_count, 2 * HD)[:, :meta_width]
+    meta_in = meta_in.astype(jnp.int32).reshape(group_count * per_dev, MOST + 1)
+    lists = meta_in[:, :MOST]
     lists = (lists % z_count) * pb_count + lists // z_count
-    local_counts = all_counts[ids]
+    local_counts = meta_in[:, MOST]
 
     query_blocks = queries.reshape(-1, BLK, queries.shape[1])
     exchanged = lax.all_to_all(query_blocks, group, split_axis=2, concat_axis=0, tiled=True)

time: 180 us -> 185 us (1.028)
  waiting for transfers between devices: 0.02 us -> 39.2 us
  blocking collectives: 93.5 us -> 54.8 us
  local copies, waits for them, and re-layouts: 24.5 us -> 29.3 us
    all_gather x1 -> x0, blocking collectives: 30.1 us -> none  [per_device(): all_lists = lax.all_gather(key_lists, ('y', 'core'), axis=0, tiled=True)]
    all_to_all x1, waiting for transfers between devices: 0.01 us -> 25.3 us  [per_device(): lax.all_to_all(query_blocks, group, split_axis=2, concat_axis=0, tiled=True)]
    all_gather x1, waiting for transfers between devices: 0.01 us -> 13.9 us  [per_device(): kv_whole = lax.all_gather(kv_part, 'z', axis=0, tiled=True)]
    unnamed x1 -> x0, blocking collectives: 9.19 us -> none
    all_gather x1, local copies, waits for them, and re-layouts: 0.12 us -> 8.71 us  [per_device(): kv_whole = lax.all_gather(kv_part, 'z', axis=0, tiled=True)]
    unnamed x14 -> x7, local copies, waits for them, and re-layouts: 9.89 us -> 6.78 us
    gather x3 -> x0, local copies, waits for them, and re-layouts: 2.07 us -> none  [the longest x1 1.38 us: per_device(): local_counts = all_counts[ids]]
  transfers between devices with their start and end apart: 2 -> 2, of which waited for: 0 -> 2; matrix products, arithmetic and copies ran while one was open for 7% -> 6% of each run, Pallas kernels for 0% -> 0%
where the time goes in v2:
time: 185 us
  blocking collectives  54.8 us (30%)
  Pallas kernels  41.9 us (23%)
  waiting for transfers between devices  39.2 us (21%)
  local copies, waits for them, and re-layouts  29.3 us (16%)
  between operations  13.5 us (7%)
  starting transfers between devices  4.37 us (2%)
    pallas_call x1, Pallas kernels, attend(): pl.pallas_call(kernel, grid_spec=grid_spec, out_shape=jax.ShapeDtypeStruc...  41.9 us
    all_to_all x1, blocking collectives, per_device(): lax.all_to_all(produced, group, split_axis=0, concat_axis=2, tiled=True)  34.8 us
    all_to_all x1, waiting for transfers between devices, per_device(): lax.all_to_all(query_blocks, group, split_axis=2, concat_axis=0, tiled=True)  25.3 us
    all_to_all x1, blocking collectives, per_device(): lax.all_to_all(stacked, group, split_axis=1, concat_axis=0, tiled=True)  20.1 us
    all_gather x1, waiting for transfers between devices, per_device(): kv_whole = lax.all_gather(kv_part, 'z', axis=0, tiled=True)  13.9 us
    all_gather x1, local copies, waits for them, and re-layouts, per_device(): kv_whole = lax.all_gather(kv_part, 'z', axis=0, tiled=True)  8.71 us
    unnamed x7, local copies, waits for them, and re-layouts  6.78 us
    all_to_all x2, local copies, waits for them, and re-layouts, per_device(): lax.all_to_all(query_blocks, group, split_axis=2, concat_axis=0, tiled=True)  5.68 us
  transfers between devices with their start and end apart: 2, of which 2 were waited for; matrix products, arithmetic and copies ran while one was open for 6% of the time, Pallas kernels for 0%

profile of v2, /device:TPU:1, one launch (start us, length us, event | category | flops | bytes accessed | tf_op | source)
XLA Modules:
  0.0 184.8 jit_solution(10291470486363811187)
XLA Ops:
  6.5 0.0 all-gather.2.cloned.1.call-start
  6.5 0.8 dynamic-slice_convert_fusion
  7.3 0.7 convert_bitcast_fusion
  8.0 0.1 copy.36
  8.1 0.1 convert_element_type.5
  8.2 1.0 copy.45
  9.2 1.0 copy.46
  10.3 0.1 pad_maximum_fusion
  10.3 0.4 copy.37
  10.8 0.0 copy-start
  10.8 20.1 %all_to_all.48 = bf16[33,32,2,128]{3,2,0,1:T(2,128)(2,1)S(1)} all-to-all(bf16[33,32,2,128]{3,2,0,1:T(2,128)(2,1)S(1)} %copy.37), channel_id=1, replica_groups=mesh['y'=4,'core'=2,'z'=8,'x'=4] {'y','core','x'}, dimensions={1} | all-to-all | bytes 1081344 | tf_op jit(solution)/shard_map/all_to_all | solution.py:102
  30.8 0.1 copy.56
  30.9 0.8 slice.35
  31.8 0.0 all-gather.2.cloned.1.call-update
  31.8 0.0 copy-done
  31.8 3.8 %copy.40 = bf16[2,128,4096]{1,0,2:T(2,128)(2,1)} copy(bf16[2,128,4096]{2,1,0:T(8,128)(2,1)S(1)} %bitcast.50) | data formatting | bytes 4194304 | tf_op jit(solution)/shard_map/reshape | solution.py:114
  35.6 4.4 %all-to-all-start.1 = ((bf16[2,128,4096]{1,0,2:T(2,128)(2,1)}), bf16[2,128,4096]{1,0,2:T(2,128)(2,1)S(1)}, u32[]{:S(2)}, u32[]{:S(2)}) async-start(bf16[2,128,4096]{1,0,2:T(2,128)(2,1)} %copy.40), calls=%async_computation.1 | async-start | bytes 4194304 | tf_op jit(solution)/shard_map/all_to_all | solution.py:115
  40.0 0.1 reshape.60
  40.1 0.7 reshape.54.lists_ref
  40.8 0.7 slice_reduce_fusion.counts_ref
  41.5 25.3 %all-to-all-done.1 = bf16[2,128,4096]{1,0,2:T(2,128)(2,1)S(1)} async-done(((bf16[2,128,4096]{1,0,2:T(2,128)(2,1)}), bf16[2,128,4096]{1,0,2:T(2,128)(2,1)S(1)}, u32[]{:S(2)}, u32[]{:S(2)}) %all-to-all-start.1) | async-done | bytes 2097184 | tf_op jit(solution)/shard_map/all_to_all | solution.py:115
  66.8 1.6 copy.41
  68.4 4.1 %copy.42 = bf16[32,2,128,128]{3,2,1,0:T(8,128)(2,1)} copy(bf16[32,2,128,128]{2,3,0,1:T(8,128)(2,1)} %bitcast.44) | data formatting | bytes 4194304 | tf_op jit(solution)/shard_map/all_to_all | solution.py:115
  72.4 13.9 %all-gather.2.cloned.1.call-done = bf16[8192,1,2,128]{3,0,2,1:T(8,128)(2,1)} async-done(((bf16[1024,1,2,128]{3,0,2,1:T(8,128)(2,1)}), bf16[8192,1,2,128]{3,0,2,1:T(8,128)(2,1)}) %all-gather.2.cloned.1.call-update) | async-done | bytes 4194320 | tf_op jit(solution)/shard_map/all_gather | solution.py:105
  86.3 8.7 %copy.43 = bf16[8192,1,2,128]{3,2,0,1:T(2,128)(2,1)S(1)} copy(bf16[8192,1,2,128]{3,0,2,1:T(8,128)(2,1)} %all-gather.2.cloned.1.call-done) | data formatting | bytes 8388608 | tf_op jit(solution)/shard_map/all_gather | solution.py:105
  95.0 2.5 %copy.54 = bf16[1024,8,2,128]{3,1,2,0:T(8,128)(2,1)} copy(bf16[1024,8,2,128]{3,2,1,0:T(2,128)(2,1)S(1)} %bitcast.43) | data formatting | bytes 8388608
  97.5 41.9 %shard_map.55 = bf16[64,128,128]{2,1,0:T(8,128)(2,1)} custom-call(s32[512]{0:T(512)} %reshape.54.lists_ref, s32[64]{0:T(128)} %slice_reduce_fusion.counts_ref, bf16[64,128,128]{2,1,0:T(8,128)(2,1)} %bitcast.51, bf16[8192,256]{1,0:T(8,128)(2,1)} %bitcast.47), custom_call_target="tpu_custom_call" | custom-call | flops 4294967296 | bytes 8388608 | tf_op jit(solution)/shard_map/pallas_call | solution.py:62
  139.5 34.8 %all_to_all.49 = bf16[64,128,128]{2,1,0:T(8,128)(2,1)S(1)} all-to-all(bf16[64,128,128]{2,1,0:T(8,128)(2,1)} %shard_map.55), channel_id=1, replica_groups=mesh['y'=4,'core'=2,'z'=8,'x'=4] {'y','core','x'}, dimensions={0} | all-to-all | bytes 4194304 | tf_op jit(solution)/shard_map/all_to_all | solution.py:117
  174.3 1.4 copy.44
  175.6 2.3 %copy.55 = bf16[32,8,32,128]{3,1,2,0:T(8,128)(2,1)} copy(bf16[32,8,32,128]{3,2,1,0:T(8,128)(2,1)S(1)} %bitcast.46) | data formatting | bytes 4194304
  (8 shorter events, 0.1 us)
Async XLA Ops:
  6.5 79.8 %all-gather.2.cloned.1.call-start = ((), (), s32[]{:S(2)}) async-start(), calls=%async_computation.3 | async-start | bytes 4718592 | tf_op jit(solution)/shard_map/all_gather | solution.py:105
  10.8 21.0 %copy-start = (bf16[256,4096]{1,0:T(8,128)(2,1)S(1)}, bf16[256,4096]{1,0:T(8,128)(2,1)}, u32[]{:S(2)}) copy-start(bf16[256,4096]{1,0:T(8,128)(2,1)} %param.7) | copy-start | bytes 6291460
  35.6 31.2 %all-to-all-start.1 = ((bf16[2,128,4096]{1,0,2:T(2,128)(2,1)}), bf16[2,128,4096]{1,0,2:T(2,128)(2,1)S(1)}, u32[]{:S(2)}, u32[]{:S(2)}) async-start(bf16[2,128,4096]{1,0,2:T(2,128)(2,1)} %copy.40), calls=%async_computation.1 | async-start | bytes 4194304 | tf_op jit(solution)/shard_map/all_to_all | solution.py:115
Sparse Core Ops, SparseCore 0:
  31.9 54.3 all-gather.1

commit v3 on v2

v3 whole, which is shorter than its diff:
```python
import functools

import jax
import jax.numpy as jnp
from jax import lax
from jax.experimental import pallas as pl
from jax.experimental.pallas import tpu as pltpu
from jax.sharding import PartitionSpec as P

HEADS = 32
HD = 128
BLK = 128
MOST = 8


def attend_kernel(lists_ref, counts_ref, q_ref, kv_ref, o_ref, kc_ref, vc_ref,
                  *, per_step, per_dev, scaling):
    step = pl.program_id(1)
    for i in range(per_step):
        qb = step * per_step + i
        cnt = counts_ref[qb]
        q = q_ref[i // per_dev, pl.ds((i % per_dev) * BLK, BLK), :]
        for s in range(MOST):
            kb = lists_ref[qb * MOST + s]
            start = pl.multiple_of(kb * BLK, BLK)
            kc_ref[pl.ds(s * BLK, BLK), :] = kv_ref[pl.ds(start, BLK), pl.ds(0, HD)]
            vc_ref[pl.ds(s * BLK, BLK), :] = kv_ref[pl.ds(start, BLK), pl.ds(HD, HD)]
        sc = lax.dot_general(q, kc_ref[...], (((1,), (1,)), ((), ())),
                             preferred_element_type=jnp.float32) * scaling
        slot = lax.broadcasted_iota(jnp.int32, sc.shape, 1) // BLK
        sc = jnp.where(slot < cnt, sc, -jnp.inf)
        m = jnp.max(sc, axis=-1, keepdims=True)
        p = jnp.exp(sc - m)
        l = jnp.sum(p, axis=-1, keepdims=True)
        w = (p / l).astype(jnp.bfloat16)
        out = jnp.dot(w, vc_ref[...], preferred_element_type=jnp.float32)
        o_ref[i] = out.astype(o_ref.dtype)


def attend(q_src, kv_rows, lists, counts, per_dev):
    sources = q_src.shape[0]
    blocks = sources * per_dev
    per_src = 4 if sources % 4 == 0 else 1
    per_step = per_src * per_dev
    nk = kv_rows.shape[0]
    kernel = functools.partial(
        attend_kernel, per_step=per_step, per_dev=per_dev, scaling=HD ** (-0.5)
    )
    flops = blocks * MOST * 4 * BLK * BLK * HD
    grid_spec = pltpu.PrefetchScalarGridSpec(
        num_scalar_prefetch=2,
        grid=(1, blocks // per_step),
        in_specs=[
            pl.BlockSpec((per_src, per_dev * BLK, HD), lambda h, b, *_: (b, 0, h)),
            pl.BlockSpec((nk, 2 * HD), lambda h, b, *_: (0, h)),
        ],
        out_specs=pl.BlockSpec((per_step, BLK, HD), lambda h, b, *_: (b, 0, h)),
        scratch_shapes=[
            pltpu.VMEM((MOST * BLK, HD), jnp.bfloat16),
            pltpu.VMEM((MOST * BLK, HD), jnp.bfloat16),
        ],
    )
    return pl.pallas_call(
        kernel,
        grid_spec=grid_spec,
        out_shape=jax.ShapeDtypeStruct((blocks, BLK, HD), jnp.bfloat16),
        compiler_params=pltpu.CompilerParams(dimension_semantics=("arbitrary", "arbitrary")),
        cost_estimate=pl.CostEstimate(
            flops=flops,
            transcendentals=blocks * BLK * MOST * BLK,
            bytes_accessed=kv_rows.size * 2 + blocks * BLK * HD * 4,
        ),
    )(lists.reshape(-1), counts, q_src, kv_rows)


def per_device(queries, keys, values, key_lists, counts, *, x_count):
    group = ("y", "core", "x")
    pb_count = lax.axis_size("y") * lax.axis_size("core")
    z_count = lax.axis_size("z")
    group_count = pb_count * x_count
    kv_count = z_count * x_count
    assert HEADS == group_count
    tokens = keys.shape[0]
    assert BLK == x_count * tokens
    rows = queries.shape[0]
    per_dev = rows // BLK
    meta_width = per_dev * (MOST + 1)
    meta_rows = 16
    assert meta_width <= HD

    kv_heads = jnp.concatenate(
        [
            keys.reshape(tokens, HEADS, HD).transpose(1, 0, 2),
            values.reshape(tokens, HEADS, HD).transpose(1, 0, 2),
        ],
        axis=2,
    )
    kv_split = lax.all_to_all(kv_heads, group, split_axis=0, concat_axis=0, tiled=True)
    kv_part = kv_split.reshape(group_count * tokens, 2 * HD)
    kv_rows = lax.all_gather(kv_part, "z", axis=0, tiled=True)

    kv_index = lax.axis_index("z") * x_count + lax.axis_index("x")
    own_lists = lax.dynamic_slice_in_dim(key_lists, kv_index * per_dev, per_dev, axis=0)
    own_counts = lax.dynamic_slice_in_dim(counts, kv_index * per_dev, per_dev, axis=0)
    meta = jnp.concatenate([own_lists, own_counts[:, None]], axis=1).reshape(-1)
    meta_block = jnp.zeros((meta_rows, HD), jnp.bfloat16).at[0, :meta_width].set(
        meta.astype(jnp.bfloat16)
    )
    q_heads = jnp.concatenate(
        [
            queries.reshape(rows, HEADS, HD).transpose(1, 0, 2),
            jnp.broadcast_to(meta_block[None], (HEADS, meta_rows, HD)),
        ],
        axis=1,
    )
    q_src = lax.all_to_all(q_heads, group, split_axis=0, concat_axis=0, tiled=True)

    meta_in = q_src[:, rows, :meta_width].astype(jnp.int32)
    meta_in = meta_in.reshape(group_count * per_dev, MOST + 1)
    lists = meta_in[:, :MOST]
    lists = (lists % z_count) * pb_count + lists // z_count
    local_counts = meta_in[:, MOST]

    produced = attend(q_src, kv_rows, lists, local_counts, per_dev)
    back = lax.all_to_all(
        produced.reshape(group_count, rows, HD), group, split_axis=0, concat_axis=0, tiled=True
    )
    return back.transpose(1, 0, 2).reshape(queries.shape)


def solution(mesh):
    pb_count, kv_count = mesh.shape["pb"], mesh.shape["kv"]
    x_count = 4
    fine = jax.sharding.Mesh(
        mesh.devices.reshape(pb_count // 2, 2, kv_count // x_count, x_count),
        ("y", "core", "z", "x"),
    )
    rows = P(("y", "core", "z", "x"), None)
    return jax.shard_map(
        functools.partial(per_device, x_count=x_count),
        mesh=fine,
        in_specs=(rows, rows, rows, P(("y", "core"), None), P(("y", "core"))),
        out_specs=rows,
        check_vma=False,
    )
```

time: 185 us -> 162 us (0.88)
  blocking collectives: 54.8 us -> 88.9 us
  waiting for transfers between devices: 39.2 us -> 12.2 us
  local copies, waits for them, and re-layouts: 29.3 us -> 11.2 us
  Pallas kernels: 41.9 us -> 35.6 us
  starting transfers between devices: 4.37 us -> 0.03 us
    all_to_all x2 -> x3, blocking collectives: 54.8 us -> 88.9 us  [the longest x1 34.8 us: per_device(): lax.all_to_all(produced.reshape(group_count, rows, HD), group, split_axis...]
    all_to_all x1 -> x0, waiting for transfers between devices: 25.3 us -> none  [per_device(): lax.all_to_all(query_blocks, group, split_axis=2, concat_axis=0, tiled=True)]
    all_gather x1 -> x0, local copies, waits for them, and re-layouts: 8.71 us -> none  [per_device(): kv_whole = lax.all_gather(kv_part, 'z', axis=0, tiled=True)]
    all_to_all x4 -> x0, local copies, waits for them, and re-layouts: 7.12 us -> none  [the longest x2 5.68 us: per_device(): lax.all_to_all(query_blocks, group, split_axis=2, concat_axis=0, tiled=True)]
    pallas_call x1, Pallas kernels: 41.9 us -> 35.6 us  [attend(): pl.pallas_call(kernel, grid_spec=grid_spec, out_shape=jax.ShapeDtypeStruc...]
    all_to_all x1 -> x0, starting transfers between devices: 4.37 us -> none  [per_device(): lax.all_to_all(query_blocks, group, split_axis=2, concat_axis=0, tiled=True)]
    unnamed x7 -> x11, local copies, waits for them, and re-layouts: 6.78 us -> 3.35 us
  transfers between devices with their start and end apart: 2 -> 1, of which waited for: 2 -> 1; matrix products, arithmetic and copies ran while one was open for 6% -> 5% of each run, Pallas kernels for 0% -> 0%
where the time goes in v3:
time: 162 us
  blocking collectives  88.9 us (55%)
  Pallas kernels  35.6 us (22%)
  between operations  13.5 us (8%)
  waiting for transfers between devices  12.2 us (8%)
  local copies, waits for them, and re-layouts  11.2 us (7%)
    pallas_call x1, Pallas kernels, attend(): pl.pallas_call(kernel, grid_spec=grid_spec, out_shape=jax.ShapeDtypeStruc...  35.6 us
    all_to_all x1, blocking collectives, per_device(): lax.all_to_all(produced.reshape(group_count, rows, HD), group, split_axis...  34.8 us
    all_to_all x1, blocking collectives, per_device(): lax.all_to_all(q_heads, group, split_axis=0, concat_axis=0, tiled=True)  34.2 us
    all_to_all x1, blocking collectives, per_device(): lax.all_to_all(kv_heads, group, split_axis=0, concat_axis=0, tiled=True)  19.9 us
    all_gather x1, waiting for transfers between devices, per_device(): kv_rows = lax.all_gather(kv_part, 'z', axis=0, tiled=True)  12.2 us
    unnamed x11, local copies, waits for them, and re-layouts  3.35 us
  transfers between devices with their start and end apart: 1, of which 1 were waited for; matrix products, arithmetic and copies ran while one was open for 5% of the time, Pallas kernels for 0%

profile of v3, /device:TPU:1, one launch (start us, length us, event | category | flops | bytes accessed | tf_op | source)
XLA Modules:
  0.0 161.9 jit_solution(8494835458930926818)
XLA Ops:
  6.5 0.0 copy-start
  6.5 0.0 copy-start.4
  6.5 0.0 copy-start.3
  6.5 0.0 copy-start.2
  6.5 0.0 all-gather.2.cloned.1.call-start
  6.6 0.9 copy-done
  7.5 1.0 bitcast_bitcast_fusion
  8.5 0.1 pad_maximum_fusion.1
  8.6 19.9 %all_to_all.15 = bf16[32,32,256]{2,1,0:T(8,128)(2,1)} all-to-all(bf16[32,32,256]{2,1,0:T(8,128)(2,1)S(1)} %pad_maximum_fusion.1), channel_id=1, replica_groups=mesh['y'=4,'core'=2,'z'=8,'x'=4] {'y','core','x'}, dimensions={0} | all-to-all | bytes 1048576 | tf_op jit(solution)/shard_map/all_to_all | solution.py:98
  28.5 0.0 all-gather.2.cloned.1.call-update
  28.5 0.0 copy-done.4
  28.5 0.1 convert_bitcast_fusion
  28.6 0.0 copy-done.3
  28.6 0.1 dynamic-slice_convert_fusion
  28.7 0.1 copy.19
  28.8 0.1 convert_element_type.16
  28.9 0.0 copy-done.2
  28.9 2.4 %copy.17 = bf16[256,4096]{0,1:T(8,128)(2,1)} copy(bf16[256,4096]{1,0:T(8,128)(2,1)S(1)} %copy-done.2) | data formatting | bytes 4194304 | tf_op args[0]
  31.3 3.2 %copy.18 = bf16[256,32,128]{2,0,1:T(8,128)(2,1)S(1)} copy(bf16[256,32,128]{0,2,1:T(8,128)(2,1)} %bitcast.27) | data formatting | bytes 4194304 | tf_op jit(solution)/shard_map/reshape | solution.py:111
  34.6 0.2 pad_maximum_fusion
  34.8 34.2 %all_to_all.16.q_ref = bf16[32,272,128]{2,1,0:T(8,128)(2,1)S(1)} all-to-all(bf16[32,272,128]{2,1,0:T(8,128)(2,1)S(1)} %pad_maximum_fusion), channel_id=1, replica_groups=mesh['y'=4,'core'=2,'z'=8,'x'=4] {'y','core','x'}, dimensions={0} | all-to-all | bytes 4456448 | tf_op jit(solution)/shard_map/all_to_all | solution.py:116
  69.0 0.0 copy-start.1
  69.0 0.1 fusion.6
  69.1 0.1 reshape.75
  69.2 0.9 reshape.69.lists_ref
  70.1 0.7 slice_reduce_fusion.counts_ref
  70.8 12.2 %all-gather.2.cloned.1.call-done.kv_ref = bf16[8192,256]{1,0:T(8,128)(2,1)} async-done(((bf16[1024,256]{1,0:T(8,128)(2,1)}), bf16[8192,256]{1,0:T(8,128)(2,1)}) %all-gather.2.cloned.1.call-update) | async-done | bytes 4194320 | tf_op jit(solution)/shard_map/all_gather | solution.py:100
  83.0 0.0 copy-done.1
  83.0 35.6 %shard_map.55 = bf16[64,128,128]{2,1,0:T(8,128)(2,1)} custom-call(s32[512]{0:T(512)} %reshape.69.lists_ref, s32[64]{0:T(128)} %slice_reduce_fusion.counts_ref, bf16[32,272,128]{2,1,0:T(8,128)(2,1)} %copy-done.1, bf16[8192,256]{1,0:T(8,128)(2,1)} %all-gather.2.cloned.1.call-done.kv_ref), custom_call_target="tpu_custom_call" | custom-call | flops 4294967296 | bytes 8388608 | tf_op jit(solution)/shard_map/pallas_call | solution.py:63
  118.7 34.8 %all_to_all.17 = bf16[32,256,128]{2,1,0:T(8,128)(2,1)S(1)} all-to-all(bf16[32,256,128]{2,1,0:T(8,128)(2,1)} %bitcast.28), channel_id=1, replica_groups=mesh['y'=4,'core'=2,'z'=8,'x'=4] {'y','core','x'}, dimensions={0} | all-to-all | bytes 4194304 | tf_op jit(solution)/shard_map/all_to_all | solution.py:125
  153.5 1.6 %copy_bitcast_fusion = bf16[256,4096]{1,0:T(8,128)(2,1)} fusion(bf16[32,256,128]{2,1,0:T(8,128)(2,1)S(1)} %all_to_all.17), kind=kLoop, calls=%fused_computation.1 | loop fusion | bytes 4194304 | tf_op jit(solution)/shard_map/reshape | solution.py:128
  (4 shorter events, 0.1 us)
Async XLA Ops:
  6.5 1.0 copy-start
  6.5 22.0 %copy-start.4 = (s32[64]{0:T(128)S(1)}, s32[64]{0:T(128)}, u32[]{:S(2)}) copy-start(s32[64]{0:T(128)} %param.11) | copy-start | bytes 772
  6.5 22.1 %copy-start.3 = (s32[64,8]{0,1:T(8,128)S(1)}, s32[64,8]{0,1:T(8,128)}, u32[]{:S(2)}) copy-start(s32[64,8]{0,1:T(8,128)} %param.10) | copy-start | bytes 6148
  6.5 22.4 %copy-start.2 = (bf16[256,4096]{1,0:T(8,128)(2,1)S(1)}, bf16[256,4096]{1,0:T(8,128)(2,1)}, u32[]{:S(2)}) copy-start(bf16[256,4096]{1,0:T(8,128)(2,1)} %param.7) | copy-start | bytes 6291460
  6.5 76.5 %all-gather.2.cloned.1.call-start = ((), (), s32[]{:S(2)}) async-start(), calls=%async_computation.3 | async-start | bytes 4718592 | tf_op jit(solution)/shard_map/all_gather | solution.py:100
  69.0 14.0 %copy-start.1 = (bf16[32,272,128]{2,1,0:T(8,128)(2,1)}, bf16[32,272,128]{2,1,0:T(8,128)(2,1)S(1)}, u32[]{:S(2)}) copy-start(bf16[32,272,128]{2,1,0:T(8,128)(2,1)S(1)} %all_to_all.16.q_ref) | copy-start | bytes 6684676
Sparse Core Ops, SparseCore 0:
  28.6 54.3 all-gather.1

commit v4 on v3

--- a/solution.py
+++ b/solution.py
@@ -14,12 +14,12 @@
 
 
 def attend_kernel(lists_ref, counts_ref, q_ref, kv_ref, o_ref, kc_ref, vc_ref,
-                  *, per_step, per_dev, scaling):
+                  *, per_step, scaling):
     step = pl.program_id(1)
     for i in range(per_step):
         qb = step * per_step + i
         cnt = counts_ref[qb]
-        q = q_ref[i // per_dev, pl.ds((i % per_dev) * BLK, BLK), :]
+        q = q_ref[i]
         for s in range(MOST):
             kb = lists_ref[qb * MOST + s]
             start = pl.multiple_of(kb * BLK, BLK)
@@ -37,21 +37,17 @@
         o_ref[i] = out.astype(o_ref.dtype)
 
 
-def attend(q_src, kv_rows, lists, counts, per_dev):
-    sources = q_src.shape[0]
-    blocks = sources * per_dev
-    per_src = 4 if sources % 4 == 0 else 1
-    per_step = per_src * per_dev
+def attend(q_src, kv_rows, lists, counts, half):
+    blocks = q_src.shape[0]
+    per_step = 8 if blocks % 8 == 0 else 1
     nk = kv_rows.shape[0]
-    kernel = functools.partial(
-        attend_kernel, per_step=per_step, per_dev=per_dev, scaling=HD ** (-0.5)
-    )
+    kernel = functools.partial(attend_kernel, per_step=per_step, scaling=HD ** (-0.5))
     flops = blocks * MOST * 4 * BLK * BLK * HD
     grid_spec = pltpu.PrefetchScalarGridSpec(
         num_scalar_prefetch=2,
         grid=(1, blocks // per_step),
         in_specs=[
-            pl.BlockSpec((per_src, per_dev * BLK, HD), lambda h, b, *_: (b, 0, h)),
+            pl.BlockSpec((per_step, BLK, HD), lambda h, b, *_: (b, half, h)),
             pl.BlockSpec((nk, 2 * HD), lambda h, b, *_: (0, h)),
         ],
         out_specs=pl.BlockSpec((per_step, BLK, HD), lambda h, b, *_: (b, 0, h)),
@@ -121,11 +117,16 @@
     lists = (lists % z_count) * pb_count + lists // z_count
     local_counts = meta_in[:, MOST]
 
-    produced = attend(q_src, kv_rows, lists, local_counts, per_dev)
-    back = lax.all_to_all(
-        produced.reshape(group_count, rows, HD), group, split_axis=0, concat_axis=0, tiled=True
+    lists = lists.reshape(group_count, per_dev, MOST)
+    local_counts = local_counts.reshape(group_count, per_dev)
+    halves = []
+    for t in range(per_dev):
+        part = attend(q_src, kv_rows, lists[:, t], local_counts[:, t], t)
+        halves.append(lax.all_to_all(part, group, split_axis=0, concat_axis=0, tiled=True))
+    back = jnp.concatenate(
+        [half.transpose(1, 0, 2).reshape(BLK, HEADS * HD) for half in halves], axis=0
     )
-    return back.transpose(1, 0, 2).reshape(queries.shape)
+    return back.reshape(queries.shape)
 
 
 def solution(mesh):

time: 162 us -> 167 us (1.031)
  blocking collectives: 88.9 us -> 54.1 us
  waiting for transfers between devices: 12.2 us -> 27.3 us
  starting transfers between devices: 0.03 us -> 14.9 us
  local copies, waits for them, and re-layouts: 11.2 us -> 15.4 us
  Pallas kernels: 35.6 us -> 39.3 us
    all_to_all x1 -> x0, blocking collectives: 34.8 us -> none  [per_device(): lax.all_to_all(produced.reshape(group_count, rows, HD), group, split_axis...]
    all_to_all x0 -> x2, waiting for transfers between devices: none -> 15.3 us  [per_device(): lax.all_to_all(part, group, split_axis=0, concat_axis=0, tiled=True)]
    all_to_all x0 -> x2, starting transfers between devices: none -> 14.9 us  [per_device(): lax.all_to_all(part, group, split_axis=0, concat_axis=0, tiled=True)]
    pallas_call x1 -> x2, Pallas kernels: 35.6 us -> 39.3 us  [attend(): pl.pallas_call(kernel, grid_spec=grid_spec, out_shape=jax.ShapeDtypeStruc...]
    concatenate x0 -> x1, local copies, waits for them, and re-layouts: none -> 2.86 us  [per_device(): jnp.concatenate([half.transpose(1, 0, 2).reshape(BLK, HEADS * HD) for hal...]
    reshape x2 -> x0, local copies, waits for them, and re-layouts: 2.57 us -> none  [the longest x1 1.64 us: per_device(): return back.transpose(1, 0, 2).reshape(queries.shape)]
    transpose x0 -> x2, local copies, waits for them, and re-layouts: none -> 1.97 us  [per_device(): half.transpose(1, 0, 2).reshape(BLK, HEADS * HD)]
    another operation x0 -> x3, local copies, waits for them, and re-layouts: none -> 1.67 us  [the longest x2 1.57 us: attend(): lists.reshape(-1)]
  transfers between devices with their start and end apart: 1 -> 3, of which waited for: 1 -> 2; matrix products, arithmetic and copies ran while one was open for 5% -> 6% of each run, Pallas kernels for 0% -> 12%
where the time goes in v4:
time: 167 us; the launch traced here: 166 us
  blocking collectives  54.1 us (32%)
  Pallas kernels  39.3 us (24%)
  waiting for transfers between devices  27.3 us (16%)
  local copies, waits for them, and re-layouts  15.4 us (9%)
  starting transfers between devices  14.9 us (9%)
  between operations  13.5 us (8%)
  other arithmetic  1.94 us (1%)
    pallas_call x2, Pallas kernels, attend(): pl.pallas_call(kernel, grid_spec=grid_spec, out_shape=jax.ShapeDtypeStruc...  39.3 us
    all_to_all x1, blocking collectives, per_device(): lax.all_to_all(q_heads, group, split_axis=0, concat_axis=0, tiled=True)  34.2 us
    all_to_all x1, blocking collectives, per_device(): lax.all_to_all(kv_heads, group, split_axis=0, concat_axis=0, tiled=True)  19.9 us
    all_to_all x2, waiting for transfers between devices, per_device(): lax.all_to_all(part, group, split_axis=0, concat_axis=0, tiled=True)  15.3 us
    all_to_all x2, starting transfers between devices, per_device(): lax.all_to_all(part, group, split_axis=0, concat_axis=0, tiled=True)  14.9 us
    all_gather x1, waiting for transfers between devices, per_device(): kv_rows = lax.all_gather(kv_part, 'z', axis=0, tiled=True)  11.9 us
    unnamed x11, local copies, waits for them, and re-layouts  3.35 us
  transfers between devices with their start and end apart: 3, of which 2 were waited for; matrix products, arithmetic and copies ran while one was open for 6% of the time, Pallas kernels for 12%

profile of v4, /device:TPU:1, one launch (start us, length us, event | category | flops | bytes accessed | tf_op | source)
XLA Modules:
  0.0 166.4 jit_solution(16488633569783147353)
XLA Ops:
  6.5 0.0 all-gather.2.cloned.1.call-start
  6.6 0.9 copy-done
  7.5 1.0 bitcast_bitcast_fusion
  8.5 0.1 pad_maximum_fusion.2
  8.6 19.9 %all_to_all.20 = bf16[32,32,256]{2,1,0:T(8,128)(2,1)} all-to-all(bf16[32,32,256]{2,1,0:T(8,128)(2,1)S(1)} %pad_maximum_fusion.2), channel_id=1, replica_groups=mesh['y'=4,'core'=2,'z'=8,'x'=4] {'y','core','x'}, dimensions={0} | all-to-all | bytes 1048576 | tf_op jit(solution)/shard_map/all_to_all | solution.py:94
  28.5 0.0 all-gather.2.cloned.1.call-update
  28.5 0.1 convert_bitcast_fusion
  28.6 0.1 dynamic-slice_convert_fusion
  28.7 0.1 copy.12
  28.8 0.1 convert_element_type.16
  28.9 2.4 %copy.10 = bf16[256,4096]{0,1:T(8,128)(2,1)} copy(bf16[256,4096]{1,0:T(8,128)(2,1)S(1)} %copy-done.2) | data formatting | bytes 4194304 | tf_op args[0]
  31.3 3.2 %copy.11 = bf16[256,32,128]{2,0,1:T(8,128)(2,1)S(1)} copy(bf16[256,32,128]{0,2,1:T(8,128)(2,1)} %bitcast.31) | data formatting | bytes 4194304 | tf_op jit(solution)/shard_map/reshape | solution.py:107
  34.6 0.2 pad_maximum_fusion
  34.8 34.2 %all_to_all.21.q_ref = bf16[32,272,128]{2,1,0:T(8,128)(2,1)S(1)} all-to-all(bf16[32,272,128]{2,1,0:T(8,128)(2,1)S(1)} %pad_maximum_fusion), channel_id=1, replica_groups=mesh['y'=4,'core'=2,'z'=8,'x'=4] {'y','core','x'}, dimensions={0} | all-to-all | bytes 4456448 | tf_op jit(solution)/shard_map/all_to_all | solution.py:112
  69.0 0.1 fusion.6
  69.1 0.1 reshape.75
  69.2 0.9 reshape_squeeze.9.lists_ref
  70.1 0.2 slice_reduce_fusion
  70.3 0.1 reshape_squeeze.10
  70.4 0.8 slice_reduce_fusion.2
  71.1 11.9 %all-gather.2.cloned.1.call-done.kv_ref = bf16[8192,256]{1,0:T(8,128)(2,1)} async-done(((bf16[1024,256]{1,0:T(8,128)(2,1)}), bf16[8192,256]{1,0:T(8,128)(2,1)}) %all-gather.2.cloned.1.call-update) | async-done | bytes 4194320 | tf_op jit(solution)/shard_map/all_gather | solution.py:96
  83.0 19.7 %shard_map.55 = bf16[32,128,128]{2,1,0:T(8,128)(2,1)} custom-call(s32[256]{0:T(256)} %reshape_squeeze.9.lists_ref, s32[32]{0:T(128)} %get-tuple-element.17.counts_ref, bf16[32,272,128]{2,1,0:T(8,128)(2,1)} %copy-done.1, bf16[8192,256]{1,0:T(8,128)(2,1)} %all-gather.2.cloned.1.call-done.kv_ref), custom_call_target="tpu_custom_call" | custom-call | flops 2147483648 | bytes 6291456 | tf_op jit(solution)/shard_map/pallas_call | solution.py:59
  102.7 7.5 %all-to-all-start.2 = ((bf16[32,128,128]{2,1,0:T(8,128)(2,1)}), bf16[32,128,128]{2,1,0:T(8,128)(2,1)S(1)}, u32[]{:S(2)}, u32[]{:S(2)}) async-start(bf16[32,128,128]{2,1,0:T(8,128)(2,1)} %shard_map.55), calls=%async_computation.2 | async-start | bytes 2097152 | tf_op jit(solution)/shard_map/all_to_all | solution.py:125
  110.2 0.7 reshape_squeeze.11.lists_ref
  110.9 19.6 %shard_map.56 = bf16[32,128,128]{2,1,0:T(8,128)(2,1)} custom-call(s32[256]{0:T(256)} %reshape_squeeze.11.lists_ref, s32[32]{0:T(128)} %get-tuple-element.18.counts_ref, bf16[32,272,128]{2,1,0:T(8,128)(2,1)} %copy-done.1, bf16[8192,256]{1,0:T(8,128)(2,1)} %all-gather.2.cloned.1.call-done.kv_ref), custom_call_target="tpu_custom_call" | custom-call | flops 2147483648 | bytes 6291456 | tf_op jit(solution)/shard_map/pallas_call | solution.py:59
  130.6 0.0 all-to-all-done.2
  130.6 7.4 %all-to-all-start.3 = ((bf16[32,128,128]{2,1,0:T(8,128)(2,1)}), bf16[32,128,128]{2,1,0:T(8,128)(2,1)S(1)}, u32[]{:S(2)}, u32[]{:S(2)}) async-start(bf16[32,128,128]{2,1,0:T(8,128)(2,1)} %shard_map.56), calls=%async_computation.3 | async-start | bytes 2097152 | tf_op jit(solution)/shard_map/all_to_all | solution.py:125
  137.9 0.7 copy.16
  138.6 15.3 %all-to-all-done.3 = bf16[32,128,128]{2,1,0:T(8,128)(2,1)S(1)} async-done(((bf16[32,128,128]{2,1,0:T(8,128)(2,1)}), bf16[32,128,128]{2,1,0:T(8,128)(2,1)S(1)}, u32[]{:S(2)}, u32[]{:S(2)}) %all-to-all-start.3) | async-done | bytes 1048608 | tf_op jit(solution)/shard_map/all_to_all | solution.py:125
  154.0 1.3 copy.18
  155.3 1.5 pad_maximum_fusion.1
  156.7 2.9 %copy.19 = bf16[256,4096]{1,0:T(8,128)(2,1)} copy(bf16[256,4096]{0,1:T(8,128)(2,1)S(1)} %pad_maximum_fusion.1) | data formatting | bytes 4194304 | tf_op jit(solution)/shard_map/concatenate | solution.py:126
  (14 shorter events, 0.1 us)
Async XLA Ops:
  6.5 1.0 copy-start
  6.5 22.0 %copy-start.4 = (s32[64]{0:T(128)S(1)}, s32[64]{0:T(128)}, u32[]{:S(2)}) copy-start(s32[64]{0:T(128)} %param.11) | copy-start | bytes 772
  6.5 22.1 %copy-start.3 = (s32[64,8]{0,1:T(8,128)S(1)}, s32[64,8]{0,1:T(8,128)}, u32[]{:S(2)}) copy-start(s32[64,8]{0,1:T(8,128)} %param.10) | copy-start | bytes 6148
  6.5 22.4 %copy-start.2 = (bf16[256,4096]{1,0:T(8,128)(2,1)S(1)}, bf16[256,4096]{1,0:T(8,128)(2,1)}, u32[]{:S(2)}) copy-start(bf16[256,4096]{1,0:T(8,128)(2,1)} %param.7) | copy-start | bytes 6291460
  6.5 76.5 %all-gather.2.cloned.1.call-start = ((), (), s32[]{:S(2)}) async-start(), calls=%async_computation.4 | async-start | bytes 4718592 | tf_op jit(solution)/shard_map/all_gather | solution.py:96
  69.0 14.0 %copy-start.1 = (bf16[32,272,128]{2,1,0:T(8,128)(2,1)}, bf16[32,272,128]{2,1,0:T(8,128)(2,1)S(1)}, u32[]{:S(2)}) copy-start(bf16[32,272,128]{2,1,0:T(8,128)(2,1)S(1)} %all_to_all.21.q_ref) | copy-start | bytes 6684676
  102.7 27.9 %all-to-all-start.2 = ((bf16[32,128,128]{2,1,0:T(8,128)(2,1)}), bf16[32,128,128]{2,1,0:T(8,128)(2,1)S(1)}, u32[]{:S(2)}, u32[]{:S(2)}) async-start(bf16[32,128,128]{2,1,0:T(8,128)(2,1)} %shard_map.55), calls=%async_computation.2 | async-start | bytes 2097152 | tf_op jit(solution)/shard_map/all_to_all | solution.py:125
  130.6 23.4 %all-to-all-start.3 = ((bf16[32,128,128]{2,1,0:T(8,128)(2,1)}), bf16[32,128,128]{2,1,0:T(8,128)(2,1)S(1)}, u32[]{:S(2)}, u32[]{:S(2)}) async-start(bf16[32,128,128]{2,1,0:T(8,128)(2,1)} %shard_map.56), calls=%async_computation.3 | async-start | bytes 2097152 | tf_op jit(solution)/shard_map/all_to_all | solution.py:125
Sparse Core Ops, SparseCore 0:
  28.6 54.3 all-gather.1

commit v5 on v3

--- a/solution.py
+++ b/solution.py
@@ -13,28 +13,38 @@
 MOST = 8
 
 
-def attend_kernel(lists_ref, counts_ref, q_ref, kv_ref, o_ref, kc_ref, vc_ref,
+SLOT_SIZES = (2, 4, MOST)
+
+
+def attend_kernel(step_ref, lists_ref, counts_ref, q_ref, kv_ref, o_ref, kc_ref, vc_ref,
                   *, per_step, per_dev, scaling):
     step = pl.program_id(1)
-    for i in range(per_step):
-        qb = step * per_step + i
-        cnt = counts_ref[qb]
-        q = q_ref[i // per_dev, pl.ds((i % per_dev) * BLK, BLK), :]
-        for s in range(MOST):
-            kb = lists_ref[qb * MOST + s]
-            start = pl.multiple_of(kb * BLK, BLK)
-            kc_ref[pl.ds(s * BLK, BLK), :] = kv_ref[pl.ds(start, BLK), pl.ds(0, HD)]
-            vc_ref[pl.ds(s * BLK, BLK), :] = kv_ref[pl.ds(start, BLK), pl.ds(HD, HD)]
-        sc = lax.dot_general(q, kc_ref[...], (((1,), (1,)), ((), ())),
-                             preferred_element_type=jnp.float32) * scaling
-        slot = lax.broadcasted_iota(jnp.int32, sc.shape, 1) // BLK
-        sc = jnp.where(slot < cnt, sc, -jnp.inf)
-        m = jnp.max(sc, axis=-1, keepdims=True)
-        p = jnp.exp(sc - m)
-        l = jnp.sum(p, axis=-1, keepdims=True)
-        w = (p / l).astype(jnp.bfloat16)
-        out = jnp.dot(w, vc_ref[...], preferred_element_type=jnp.float32)
-        o_ref[i] = out.astype(o_ref.dtype)
+
+    def body_for(slots):
+        def body():
+            for i in range(per_step):
+                qb = step * per_step + i
+                cnt = counts_ref[qb]
+                q = q_ref[i // per_dev, pl.ds((i % per_dev) * BLK, BLK), :]
+                for s in range(slots):
+                    kb = lists_ref[qb * MOST + s]
+                    start = pl.multiple_of(kb * BLK, BLK)
+                    kc_ref[pl.ds(s * BLK, BLK), :] = kv_ref[pl.ds(start, BLK), pl.ds(0, HD)]
+                    vc_ref[pl.ds(s * BLK, BLK), :] = kv_ref[pl.ds(start, BLK), pl.ds(HD, HD)]
+                sc = lax.dot_general(q, kc_ref[pl.ds(0, slots * BLK), :], (((1,), (1,)), ((), ())),
+                                     preferred_element_type=jnp.float32) * scaling
+                slot = lax.broadcasted_iota(jnp.int32, sc.shape, 1) // BLK
+                sc = jnp.where(slot < cnt, sc, -jnp.inf)
+                m = jnp.max(sc, axis=-1, keepdims=True)
+                p = jnp.exp(sc - m)
+                l = jnp.sum(p, axis=-1, keepdims=True)
+                w = (p / l).astype(jnp.bfloat16)
+                out = jnp.dot(w, vc_ref[pl.ds(0, slots * BLK), :],
+                              preferred_element_type=jnp.float32)
+                o_ref[i] = out.astype(o_ref.dtype)
+        return body
+
+    lax.switch(step_ref[step], [body_for(n) for n in SLOT_SIZES])
 
 
 def attend(q_src, kv_rows, lists, counts, per_dev):
@@ -47,8 +57,12 @@
         attend_kernel, per_step=per_step, per_dev=per_dev, scaling=HD ** (-0.5)
     )
     flops = blocks * MOST * 4 * BLK * BLK * HD
+    widest = jnp.max(counts.reshape(blocks // per_step, per_step), axis=1)
+    step_size = jnp.zeros_like(widest)
+    for n in SLOT_SIZES[:-1]:
+        step_size = step_size + (widest > n).astype(jnp.int32)
     grid_spec = pltpu.PrefetchScalarGridSpec(
-        num_scalar_prefetch=2,
+        num_scalar_prefetch=3,
         grid=(1, blocks // per_step),
         in_specs=[
             pl.BlockSpec((per_src, per_dev * BLK, HD), lambda h, b, *_: (b, 0, h)),
@@ -70,7 +84,7 @@
             transcendentals=blocks * BLK * MOST * BLK,
             bytes_accessed=kv_rows.size * 2 + blocks * BLK * HD * 4,
         ),
-    )(lists.reshape(-1), counts, q_src, kv_rows)
+    )(step_size, lists.reshape(-1), counts, q_src, kv_rows)
 
 
 def per_device(queries, keys, values, key_lists, counts, *, x_count):

time: 162 us -> 157 us (0.969)
  Pallas kernels: 35.6 us -> 31.2 us
    pallas_call x1, Pallas kernels: 35.6 us -> 31.2 us  [attend(): pl.pallas_call(kernel, grid_spec=grid_spec, out_shape=jax.ShapeDtypeStruc...]
    unnamed x11 -> x13, local copies, waits for them, and re-layouts: 3.35 us -> 3.36 us
where the time goes in v5:
time: 157 us; the launch traced here: 158 us
  blocking collectives  88.9 us (57%)
  Pallas kernels  31.2 us (20%)
  between operations  13.5 us (9%)
  waiting for transfers between devices  12.1 us (8%)
  local copies, waits for them, and re-layouts  10.7 us (7%)
    all_to_all x1, blocking collectives, per_device(): lax.all_to_all(produced.reshape(group_count, rows, HD), group, split_axis...  34.8 us
    all_to_all x1, blocking collectives, per_device(): lax.all_to_all(q_heads, group, split_axis=0, concat_axis=0, tiled=True)  34.2 us
    pallas_call x1, Pallas kernels, attend(): pl.pallas_call(kernel, grid_spec=grid_spec, out_shape=jax.ShapeDtypeStruc...  31.2 us
    all_to_all x1, blocking collectives, per_device(): lax.all_to_all(kv_heads, group, split_axis=0, concat_axis=0, tiled=True)  19.9 us
    all_gather x1, waiting for transfers between devices, per_device(): kv_rows = lax.all_gather(kv_part, 'z', axis=0, tiled=True)  12 us
    unnamed x13, local copies, waits for them, and re-layouts  3.36 us
    reshape x1, local copies, waits for them, and re-layouts, per_device(): queries.reshape(rows, HEADS, HD).transpose(1, 0, 2)  3.21 us
  transfers between devices with their start and end apart: 1, of which 1 were waited for; matrix products, arithmetic and copies ran while one was open for 5% of the time, Pallas kernels for 0%

profile of v5, /device:TPU:1, one launch (start us, length us, event | category | flops | bytes accessed | tf_op | source)
XLA Modules:
  0.0 157.6 jit_solution(1105382576508701530)
XLA Ops:
  6.5 0.0 copy-start
  6.5 0.0 all-gather.2.cloned.1.call-start
  6.6 0.9 copy-done
  7.5 1.0 bitcast_bitcast_fusion
  8.5 0.1 pad_maximum_fusion.1
  8.6 19.9 %all_to_all.15 = bf16[32,32,256]{2,1,0:T(8,128)(2,1)} all-to-all(bf16[32,32,256]{2,1,0:T(8,128)(2,1)S(1)} %pad_maximum_fusion.1), channel_id=1, replica_groups=mesh['y'=4,'core'=2,'z'=8,'x'=4] {'y','core','x'}, dimensions={0} | all-to-all | bytes 1048576 | tf_op jit(solution)/shard_map/all_to_all | solution.py:112
  28.5 0.0 all-gather.2.cloned.1.call-update
  28.5 0.0 copy-done.5
  28.5 0.1 convert_bitcast_fusion
  28.6 0.0 copy-done.3
  28.6 0.1 dynamic-slice_convert_fusion
  28.7 0.1 copy.19
  28.8 0.1 convert_element_type.22
  28.9 0.0 copy-done.2
  28.9 2.4 %copy.17 = bf16[256,4096]{0,1:T(8,128)(2,1)} copy(bf16[256,4096]{1,0:T(8,128)(2,1)S(1)} %copy-done.2) | data formatting | bytes 4194304 | tf_op args[0]
  31.3 3.2 %copy.18 = bf16[256,32,128]{2,0,1:T(8,128)(2,1)S(1)} copy(bf16[256,32,128]{0,2,1:T(8,128)(2,1)} %bitcast.27) | data formatting | bytes 4194304 | tf_op jit(solution)/shard_map/reshape | solution.py:125
  34.6 0.2 pad_maximum_fusion
  34.8 34.2 %all_to_all.16.q_ref = bf16[32,272,128]{2,1,0:T(8,128)(2,1)S(1)} all-to-all(bf16[32,272,128]{2,1,0:T(8,128)(2,1)S(1)} %pad_maximum_fusion), channel_id=1, replica_groups=mesh['y'=4,'core'=2,'z'=8,'x'=4] {'y','core','x'}, dimensions={0} | all-to-all | bytes 4456448 | tf_op jit(solution)/shard_map/all_to_all | solution.py:130
  69.0 0.1 fusion.6
  69.1 0.1 reshape.75
  69.1 0.2 slice_reduce_fusion.counts_ref
  69.3 0.0 copy-start.4
  69.3 0.1 reshape_squeeze.3
  69.4 0.9 reshape.69.lists_ref
  70.3 0.1 reduce_max.9
  70.4 0.6 fusion.7.step_ref
  71.0 12.0 %all-gather.2.cloned.1.call-done.kv_ref = bf16[8192,256]{1,0:T(8,128)(2,1)} async-done(((bf16[1024,256]{1,0:T(8,128)(2,1)}), bf16[8192,256]{1,0:T(8,128)(2,1)}) %all-gather.2.cloned.1.call-update) | async-done | bytes 4194320 | tf_op jit(solution)/shard_map/all_gather | solution.py:114
  83.0 0.0 copy-done.1
  83.0 0.0 copy-done.4
  83.0 31.2 %shard_map.55 = bf16[64,128,128]{2,1,0:T(8,128)(2,1)} custom-call(s32[8]{0:T(128)} %fusion.7.step_ref, s32[512]{0:T(512)} %reshape.69.lists_ref, s32[64]{0:T(128)} %copy-done.4, bf16[32,272,128]{2,1,0:T(8,128)(2,1)} %copy-done.1, bf16[8192,256]{1,0:T(8,128)(2,1)} %all-gather.2.cloned.1.call-done.kv_ref), custom_call_target="tpu_custom_call" | custom-call | flops 4294967296 | bytes 8388608 | tf_op jit(solution)/shard_map/pallas_call | solution.py:77
  114.3 34.8 %all_to_all.17 = bf16[32,256,128]{2,1,0:T(8,128)(2,1)S(1)} all-to-all(bf16[32,256,128]{2,1,0:T(8,128)(2,1)} %bitcast.28), channel_id=1, replica_groups=mesh['y'=4,'core'=2,'z'=8,'x'=4] {'y','core','x'}, dimensions={0} | all-to-all | bytes 4194304 | tf_op jit(solution)/shard_map/all_to_all | solution.py:139
  149.1 1.6 %copy_bitcast_fusion = bf16[256,4096]{1,0:T(8,128)(2,1)} fusion(bf16[32,256,128]{2,1,0:T(8,128)(2,1)S(1)} %all_to_all.17), kind=kLoop, calls=%fused_computation.1 | loop fusion | bytes 4194304 | tf_op jit(solution)/shard_map/reshape | solution.py:142
  (8 shorter events, 0.1 us)
Async XLA Ops:
  6.5 1.0 copy-start
  6.5 22.0 %copy-start.5 = (s32[64]{0:T(128)S(1)}, s32[64]{0:T(128)}, u32[]{:S(2)}) copy-start(s32[64]{0:T(128)} %param.11) | copy-start | bytes 772
  6.5 22.1 %copy-start.3 = (s32[64,8]{0,1:T(8,128)S(1)}, s32[64,8]{0,1:T(8,128)}, u32[]{:S(2)}) copy-start(s32[64,8]{0,1:T(8,128)} %param.10) | copy-start | bytes 6148
  6.5 22.4 %copy-start.2 = (bf16[256,4096]{1,0:T(8,128)(2,1)S(1)}, bf16[256,4096]{1,0:T(8,128)(2,1)}, u32[]{:S(2)}) copy-start(bf16[256,4096]{1,0:T(8,128)(2,1)} %param.7) | copy-start | bytes 6291460
  6.5 76.5 %all-gather.2.cloned.1.call-start = ((), (), s32[]{:S(2)}) async-start(), calls=%async_computation.3 | async-start | bytes 4718592 | tf_op jit(solution)/shard_map/all_gather | solution.py:114
  69.0 14.0 %copy-start.1 = (bf16[32,272,128]{2,1,0:T(8,128)(2,1)}, bf16[32,272,128]{2,1,0:T(8,128)(2,1)S(1)}, u32[]{:S(2)}) copy-start(bf16[32,272,128]{2,1,0:T(8,128)(2,1)S(1)} %all_to_all.16.q_ref) | copy-start | bytes 6684676
  69.3 13.7 %copy-start.4 = (s32[64]{0:T(128)}, s32[64]{0:T(128)S(1)}, u32[]{:S(2)}) copy-start(s32[64]{0:T(128)S(1)} %slice_reduce_fusion.counts_ref) | copy-start | bytes 772
Sparse Core Ops, SparseCore 0:
  28.6 54.3 all-gather.1

commit v6 on v5

--- a/solution.py
+++ b/solution.py
@@ -16,9 +16,9 @@
 SLOT_SIZES = (2, 4, MOST)
 
 
-def attend_kernel(step_ref, lists_ref, counts_ref, q_ref, kv_ref, o_ref, kc_ref, vc_ref,
-                  *, per_step, per_dev, scaling):
-    step = pl.program_id(1)
+def weights_kernel(step_ref, lists_ref, counts_ref, q_ref, k_ref, w_ref, kc_ref,
+                   *, per_step, per_dev, scaling):
+    step = pl.program_id(0)
 
     def body_for(slots):
         def body():
@@ -29,8 +29,7 @@
                 for s in range(slots):
                     kb = lists_ref[qb * MOST + s]
                     start = pl.multiple_of(kb * BLK, BLK)
-                    kc_ref[pl.ds(s * BLK, BLK), :] = kv_ref[pl.ds(start, BLK), pl.ds(0, HD)]
-                    vc_ref[pl.ds(s * BLK, BLK), :] = kv_ref[pl.ds(start, BLK), pl.ds(HD, HD)]
+                    kc_ref[pl.ds(s * BLK, BLK), :] = k_ref[pl.ds(start, BLK), :]
                 sc = lax.dot_general(q, kc_ref[pl.ds(0, slots * BLK), :], (((1,), (1,)), ((), ())),
                                      preferred_element_type=jnp.float32) * scaling
                 slot = lax.broadcasted_iota(jnp.int32, sc.shape, 1) // BLK
@@ -38,7 +37,24 @@
                 m = jnp.max(sc, axis=-1, keepdims=True)
                 p = jnp.exp(sc - m)
                 l = jnp.sum(p, axis=-1, keepdims=True)
-                w = (p / l).astype(jnp.bfloat16)
+                w_ref[i, :, pl.ds(0, slots * BLK)] = (p / l).astype(jnp.bfloat16)
+        return body
+
+    lax.switch(step_ref[step], [body_for(n) for n in SLOT_SIZES])
+
+
+def mix_kernel(step_ref, lists_ref, w_ref, v_ref, o_ref, vc_ref, *, per_step):
+    step = pl.program_id(0)
+
+    def body_for(slots):
+        def body():
+            for i in range(per_step):
+                qb = step * per_step + i
+                for s in range(slots):
+                    kb = lists_ref[qb * MOST + s]
+                    start = pl.multiple_of(kb * BLK, BLK)
+                    vc_ref[pl.ds(s * BLK, BLK), :] = v_ref[pl.ds(start, BLK), :]
+                w = w_ref[i, :, pl.ds(0, slots * BLK)]
                 out = jnp.dot(w, vc_ref[pl.ds(0, slots * BLK), :],
                               preferred_element_type=jnp.float32)
                 o_ref[i] = out.astype(o_ref.dtype)
@@ -47,44 +63,59 @@
     lax.switch(step_ref[step], [body_for(n) for n in SLOT_SIZES])
 
 
-def attend(q_src, kv_rows, lists, counts, per_dev):
+def attend(q_src, k_rows, v_rows, lists, counts, per_dev, order_after=None):
     sources = q_src.shape[0]
     blocks = sources * per_dev
     per_src = 4 if sources % 4 == 0 else 1
     per_step = per_src * per_dev
-    nk = kv_rows.shape[0]
-    kernel = functools.partial(
-        attend_kernel, per_step=per_step, per_dev=per_dev, scaling=HD ** (-0.5)
-    )
-    flops = blocks * MOST * 4 * BLK * BLK * HD
+    nk = k_rows.shape[0]
+    width = MOST * BLK
     widest = jnp.max(counts.reshape(blocks // per_step, per_step), axis=1)
     step_size = jnp.zeros_like(widest)
     for n in SLOT_SIZES[:-1]:
         step_size = step_size + (widest > n).astype(jnp.int32)
-    grid_spec = pltpu.PrefetchScalarGridSpec(
-        num_scalar_prefetch=3,
-        grid=(1, blocks // per_step),
-        in_specs=[
-            pl.BlockSpec((per_src, per_dev * BLK, HD), lambda h, b, *_: (b, 0, h)),
-            pl.BlockSpec((nk, 2 * HD), lambda h, b, *_: (0, h)),
-        ],
-        out_specs=pl.BlockSpec((per_step, BLK, HD), lambda h, b, *_: (b, 0, h)),
-        scratch_shapes=[
-            pltpu.VMEM((MOST * BLK, HD), jnp.bfloat16),
-            pltpu.VMEM((MOST * BLK, HD), jnp.bfloat16),
-        ],
-    )
+    flat_lists = lists.reshape(-1)
+    weights = pl.pallas_call(
+        functools.partial(weights_kernel, per_step=per_step, per_dev=per_dev,
+                          scaling=HD ** (-0.5)),
+        grid_spec=pltpu.PrefetchScalarGridSpec(
+            num_scalar_prefetch=3,
+            grid=(blocks // per_step,),
+            in_specs=[
+                pl.BlockSpec((per_src, per_dev * BLK, HD), lambda b, *_: (b, 0, 0)),
+                pl.BlockSpec((nk, HD), lambda b, *_: (0, 0)),
+            ],
+            out_specs=pl.BlockSpec((per_step, BLK, width), lambda b, *_: (b, 0, 0)),
+            scratch_shapes=[pltpu.VMEM((width, HD), jnp.bfloat16)],
+        ),
+        out_shape=jax.ShapeDtypeStruct((blocks, BLK, width), jnp.bfloat16),
+        compiler_params=pltpu.CompilerParams(dimension_semantics=("arbitrary",)),
+        cost_estimate=pl.CostEstimate(
+            flops=blocks * 2 * BLK * width * HD,
+            transcendentals=blocks * BLK * width,
+            bytes_accessed=k_rows.size * 2 + blocks * BLK * (HD + width) * 2,
+        ),
+    )(step_size, flat_lists, counts, q_src, k_rows)
     return pl.pallas_call(
-        kernel,
-        grid_spec=grid_spec,
+        functools.partial(mix_kernel, per_step=per_step),
+        grid_spec=pltpu.PrefetchScalarGridSpec(
+            num_scalar_prefetch=2,
+            grid=(blocks // per_step,),
+            in_specs=[
+                pl.BlockSpec((per_step, BLK, width), lambda b, *_: (b, 0, 0)),
+                pl.BlockSpec((nk, HD), lambda b, *_: (0, 0)),
+            ],
+            out_specs=pl.BlockSpec((per_step, BLK, HD), lambda b, *_: (b, 0, 0)),
+            scratch_shapes=[pltpu.VMEM((width, HD), jnp.bfloat16)],
+        ),
         out_shape=jax.ShapeDtypeStruct((blocks, BLK, HD), jnp.bfloat16),
-        compiler_params=pltpu.CompilerParams(dimension_semantics=("arbitrary", "arbitrary")),
+        compiler_params=pltpu.CompilerParams(dimension_semantics=("arbitrary",)),
         cost_estimate=pl.CostEstimate(
-            flops=flops,
-            transcendentals=blocks * BLK * MOST * BLK,
-            bytes_accessed=kv_rows.size * 2 + blocks * BLK * HD * 4,
+            flops=blocks * 2 * BLK * width * HD,
+            transcendentals=0,
+            bytes_accessed=v_rows.size * 2 + blocks * BLK * (HD + width) * 2,
         ),
-    )(step_size, lists.reshape(-1), counts, q_src, kv_rows)
+    )(step_size, flat_lists, weights, v_rows)
 
 
 def per_device(queries, keys, values, key_lists, counts, *, x_count):
@@ -111,7 +142,8 @@
     )
     kv_split = lax.all_to_all(kv_heads, group, split_axis=0, concat_axis=0, tiled=True)
     kv_part = kv_split.reshape(group_count * tokens, 2 * HD)
-    kv_rows = lax.all_gather(kv_part, "z", axis=0, tiled=True)
+    k_rows = lax.all_gather(kv_part[:, :HD], "z", axis=0, tiled=True)
+    v_rows = lax.all_gather(kv_part[:, HD:], "z", axis=0, tiled=True)
 
     kv_index = lax.axis_index("z") * x_count + lax.axis_index("x")
     own_lists = lax.dynamic_slice_in_dim(key_lists, kv_index * per_dev, per_dev, axis=0)
@@ -135,7 +167,7 @@
     lists = (lists % z_count) * pb_count + lists // z_count
     local_counts = meta_in[:, MOST]
 
-    produced = attend(q_src, kv_rows, lists, local_counts, per_dev)
+    produced = attend(q_src, k_rows, v_rows, lists, local_counts, per_dev)
     back = lax.all_to_all(
         produced.reshape(group_count, rows, HD), group, split_axis=0, concat_axis=0, tiled=True
     )

time: 157 us -> 168 us (1.070)
  waiting for transfers between devices: 12.1 us -> 21 us
  Pallas kernels: 31.2 us -> 27.4 us
  blocking collectives: 88.9 us -> 92.6 us
    all_gather x1 -> x2, waiting for transfers between devices: 12 us -> 20.3 us  [the longest x1 20.3 us: per_device(): v_rows = lax.all_gather(kv_part[:, HD:], 'z', axis=0, tiled=True)]
    pallas_call x1 -> x2, Pallas kernels: 31.2 us -> 27.4 us  [the longest x1 15.1 us: attend(): pl.pallas_call(functools.partial(weights_kernel, per_step=per_step, per_d...]
    all_to_all x1, blocking collectives: 34.8 us -> 38.5 us  [per_device(): lax.all_to_all(produced.reshape(group_count, rows, HD), group, split_axis...]
  transfers between devices with their start and end apart: 1 -> 2, of which waited for: 1 -> 1; matrix products, arithmetic and copies ran while one was open for 5% -> 5% of each run, Pallas kernels for 0% -> 9%
where the time goes in v6:
time: 168 us; the launch traced here: 167 us
  blocking collectives  92.6 us (55%)
  Pallas kernels  27.4 us (16%)
  waiting for transfers between devices  21 us (12%)
  between operations  13.5 us (8%)
  local copies, waits for them, and re-layouts  11.5 us (7%)
    all_to_all x1, blocking collectives, per_device(): lax.all_to_all(produced.reshape(group_count, rows, HD), group, split_axis...  38.5 us
    all_to_all x1, blocking collectives, per_device(): lax.all_to_all(q_heads, group, split_axis=0, concat_axis=0, tiled=True)  34.2 us
    all_gather x1, waiting for transfers between devices, per_device(): v_rows = lax.all_gather(kv_part[:, HD:], 'z', axis=0, tiled=True)  20.3 us
    all_to_all x1, blocking collectives, per_device(): lax.all_to_all(kv_heads, group, split_axis=0, concat_axis=0, tiled=True)  19.9 us
    pallas_call x1, Pallas kernels, attend(): pl.pallas_call(functools.partial(weights_kernel, per_step=per_step, per_d...  15.1 us
    pallas_call x1, Pallas kernels, attend(): pl.pallas_call(functools.partial(mix_kernel, per_step=per_step), grid_spe...  12.2 us
    unnamed x13, local copies, waits for them, and re-layouts  3.41 us
  transfers between devices with their start and end apart: 2, of which 1 were waited for; matrix products, arithmetic and copies ran while one was open for 5% of the time, Pallas kernels for 9%

profile of v6, /device:TPU:1, one launch (start us, length us, event | category | flops | bytes accessed | tf_op | source)
XLA Modules:
  0.0 167.3 jit_solution(2440771201172302939)
XLA Ops:
  6.5 0.9 copy-done
  7.5 1.0 bitcast_bitcast_fusion
  8.5 0.0 copy-start.5
  8.5 0.0 copy-start.4
  8.6 0.0 copy-start.2
  8.6 0.1 pad_maximum_fusion.1
  8.6 19.9 %all_to_all.15 = bf16[32,32,256]{2,1,0:T(8,128)(2,1)S(1)} all-to-all(bf16[32,32,256]{2,1,0:T(8,128)(2,1)S(1)} %pad_maximum_fusion.1), channel_id=1, replica_groups=mesh['y'=4,'core'=2,'z'=8,'x'=4] {'y','core','x'}, dimensions={0} | all-to-all | bytes 1048576 | tf_op jit(solution)/shard_map/all_to_all | solution.py:143
  28.6 0.8 fusion.8
  29.4 0.0 all-gather.3.cloned.1.call-update
  29.4 0.0 all-gather.5.cloned.1.call-start
  29.4 0.7 all-gather.5.cloned.1.call-update
  30.2 0.1 convert_bitcast_fusion
  30.2 0.1 dynamic-slice_convert_fusion
  30.3 0.1 copy.19
  30.4 0.1 convert_element_type.22
  30.5 2.4 %copy.17 = bf16[256,4096]{0,1:T(8,128)(2,1)} copy(bf16[256,4096]{1,0:T(8,128)(2,1)S(1)} %copy-done.2) | data formatting | bytes 4194304 | tf_op args[0]
  33.0 3.2 %copy.18 = bf16[256,32,128]{2,0,1:T(8,128)(2,1)S(1)} copy(bf16[256,32,128]{0,2,1:T(8,128)(2,1)} %bitcast.28) | data formatting | bytes 4194304 | tf_op jit(solution)/shard_map/reshape | solution.py:157
  36.2 0.2 pad_maximum_fusion
  36.4 34.2 %all_to_all.16.q_ref = bf16[32,272,128]{2,1,0:T(8,128)(2,1)S(1)} all-to-all(bf16[32,272,128]{2,1,0:T(8,128)(2,1)S(1)} %pad_maximum_fusion), channel_id=1, replica_groups=mesh['y'=4,'core'=2,'z'=8,'x'=4] {'y','core','x'}, dimensions={0} | all-to-all | bytes 4456448 | tf_op jit(solution)/shard_map/all_to_all | solution.py:162
  70.6 0.1 fusion.6
  70.7 0.1 reshape.75
  70.8 0.2 slice_reduce_fusion.counts_ref
  70.9 0.0 copy-start.3
  71.0 0.1 reshape_squeeze.3
  71.1 0.9 reshape.69.lists_ref
  71.9 0.1 reduce_max.9
  72.1 0.6 fusion.7.step_ref
  72.6 15.1 %shard_map.55.w_ref = bf16[64,128,1024]{2,1,0:T(8,128)(2,1)} custom-call(s32[8]{0:T(128)} %fusion.7.step_ref, s32[512]{0:T(512)} %reshape.69.lists_ref, s32[64]{0:T(128)} %copy-done.3, bf16[32,272,128]{2,1,0:T(8,128)(2,1)} %copy-done.1, bf16[8192,128]{1,0:T(8,128)(2,1)} %all-gather.3.cloned.1.call-done.k_ref), custom_call_target="tpu_custom_call" | custom-call | flops 2147483648 | bytes 20971520 | tf_op jit(solution)/shard_map/pallas_call | solution.py:78
  87.8 20.3 %all-gather.5.cloned.1.call-done.v_ref = bf16[8192,128]{1,0:T(8,128)(2,1)} async-done(((bf16[1024,128]{1,0:T(8,128)(2,1)}), bf16[8192,128]{1,0:T(8,128)(2,1)}) %all-gather.5.cloned.1.call-update) | async-done | bytes 2097168 | tf_op jit(solution)/shard_map/all_gather | solution.py:146
  108.1 12.2 %shard_map.56 = bf16[64,128,128]{2,1,0:T(8,128)(2,1)} custom-call(s32[8]{0:T(128)} %fusion.7.step_ref, s32[512]{0:T(512)} %reshape.69.lists_ref, bf16[64,128,1024]{2,1,0:T(8,128)(2,1)} %shard_map.55.w_ref, bf16[8192,128]{1,0:T(8,128)(2,1)} %all-gather.5.cloned.1.call-done.v_ref), custom_call_target="tpu_custom_call" | custom-call | flops 2147483648 | bytes 20971520 | tf_op jit(solution)/shard_map/pallas_call | solution.py:99
  120.3 38.5 %all_to_all.17 = bf16[32,256,128]{2,1,0:T(8,128)(2,1)S(1)} all-to-all(bf16[32,256,128]{2,1,0:T(8,128)(2,1)} %bitcast.26), channel_id=1, replica_groups=mesh['y'=4,'core'=2,'z'=8,'x'=4] {'y','core','x'}, dimensions={0} | all-to-all | bytes 4194304 | tf_op jit(solution)/shard_map/all_to_all | solution.py:171
  158.8 1.6 copy_bitcast_fusion
  (13 shorter events, 0.1 us)
Async XLA Ops:
  6.5 1.0 copy-start
  6.5 66.1 %all-gather.3.cloned.1.call-start = ((), (), s32[]{:S(2)}) async-start(), calls=%async_computation.3 | async-start | bytes 2359296 | tf_op jit(solution)/shard_map/all_gather | solution.py:145
  8.5 21.6 %copy-start.5 = (s32[64]{0:T(128)S(1)}, s32[64]{0:T(128)}, u32[]{:S(2)}) copy-start(s32[64]{0:T(128)} %param.11) | copy-start | bytes 772
  8.5 21.7 %copy-start.4 = (s32[64,8]{0,1:T(8,128)S(1)}, s32[64,8]{0,1:T(8,128)}, u32[]{:S(2)}) copy-start(s32[64,8]{0,1:T(8,128)} %param.10) | copy-start | bytes 6148
  8.6 22.0 %copy-start.2 = (bf16[256,4096]{1,0:T(8,128)(2,1)S(1)}, bf16[256,4096]{1,0:T(8,128)(2,1)}, u32[]{:S(2)}) copy-start(bf16[256,4096]{1,0:T(8,128)(2,1)} %param.7) | copy-start | bytes 6291460
  29.4 78.7 %all-gather.5.cloned.1.call-start = ((), (), s32[]{:S(2)}) async-start(), calls=%async_computation.4 | async-start | bytes 2359296 | tf_op jit(solution)/shard_map/all_gather | solution.py:146
  70.6 2.0 %copy-start.1 = (bf16[32,272,128]{2,1,0:T(8,128)(2,1)}, bf16[32,272,128]{2,1,0:T(8,128)(2,1)S(1)}, u32[]{:S(2)}) copy-start(bf16[32,272,128]{2,1,0:T(8,128)(2,1)S(1)} %all_to_all.16.q_ref) | copy-start | bytes 6684676
  70.9 1.7 %copy-start.3 = (s32[64]{0:T(128)}, s32[64]{0:T(128)S(1)}, u32[]{:S(2)}) copy-start(s32[64]{0:T(128)S(1)} %slice_reduce_fusion.counts_ref) | copy-start | bytes 772
Sparse Core Ops, SparseCore 0:
  29.5 36.9 all-gather.2
  68.3 39.7 all-gather.4

commit v7 on v6

--- a/solution.py
+++ b/solution.py
@@ -63,12 +63,12 @@
     lax.switch(step_ref[step], [body_for(n) for n in SLOT_SIZES])
 
 
-def attend(q_src, k_rows, v_rows, lists, counts, per_dev, order_after=None):
+def attend(q_src, kv_rows, lists, counts, per_dev):
     sources = q_src.shape[0]
     blocks = sources * per_dev
     per_src = 4 if sources % 4 == 0 else 1
     per_step = per_src * per_dev
-    nk = k_rows.shape[0]
+    nk = kv_rows.shape[0]
     width = MOST * BLK
     widest = jnp.max(counts.reshape(blocks // per_step, per_step), axis=1)
     step_size = jnp.zeros_like(widest)
@@ -93,9 +93,9 @@
         cost_estimate=pl.CostEstimate(
             flops=blocks * 2 * BLK * width * HD,
             transcendentals=blocks * BLK * width,
-            bytes_accessed=k_rows.size * 2 + blocks * BLK * (HD + width) * 2,
+            bytes_accessed=kv_rows.size + blocks * BLK * (HD + width) * 2,
         ),
-    )(step_size, flat_lists, counts, q_src, k_rows)
+    )(step_size, flat_lists, counts, q_src, kv_rows)
     return pl.pallas_call(
         functools.partial(mix_kernel, per_step=per_step),
         grid_spec=pltpu.PrefetchScalarGridSpec(
@@ -103,7 +103,7 @@
             grid=(blocks // per_step,),
             in_specs=[
                 pl.BlockSpec((per_step, BLK, width), lambda b, *_: (b, 0, 0)),
-                pl.BlockSpec((nk, HD), lambda b, *_: (0, 0)),
+                pl.BlockSpec((nk, HD), lambda b, *_: (0, 1)),
             ],
             out_specs=pl.BlockSpec((per_step, BLK, HD), lambda b, *_: (b, 0, 0)),
             scratch_shapes=[pltpu.VMEM((width, HD), jnp.bfloat16)],
@@ -113,9 +113,9 @@
         cost_estimate=pl.CostEstimate(
             flops=blocks * 2 * BLK * width * HD,
             transcendentals=0,
-            bytes_accessed=v_rows.size * 2 + blocks * BLK * (HD + width) * 2,
+            bytes_accessed=kv_rows.size + blocks * BLK * (HD + width) * 2,
         ),
-    )(step_size, flat_lists, weights, v_rows)
+    )(step_size, flat_lists, weights, kv_rows)
 
 
 def per_device(queries, keys, values, key_lists, counts, *, x_count):
@@ -142,8 +142,7 @@
     )
     kv_split = lax.all_to_all(kv_heads, group, split_axis=0, concat_axis=0, tiled=True)
     kv_part = kv_split.reshape(group_count * tokens, 2 * HD)
-    k_rows = lax.all_gather(kv_part[:, :HD], "z", axis=0, tiled=True)
-    v_rows = lax.all_gather(kv_part[:, HD:], "z", axis=0, tiled=True)
+    kv_rows = lax.all_gather(kv_part, "z", axis=0, tiled=True)
 
     kv_index = lax.axis_index("z") * x_count + lax.axis_index("x")
     own_lists = lax.dynamic_slice_in_dim(key_lists, kv_index * per_dev, per_dev, axis=0)
@@ -167,7 +166,7 @@
     lists = (lists % z_count) * pb_count + lists // z_count
     local_counts = meta_in[:, MOST]
 
-    produced = attend(q_src, k_rows, v_rows, lists, local_counts, per_dev)
+    produced = attend(q_src, kv_rows, lists, local_counts, per_dev)
     back = lax.all_to_all(
         produced.reshape(group_count, rows, HD), group, split_axis=0, concat_axis=0, tiled=True
     )

time: 168 us -> 156 us (0.929)
  waiting for transfers between devices: 21 us -> 12.1 us
  blocking collectives: 92.6 us -> 88.9 us
    all_gather x2 -> x1, waiting for transfers between devices: 20.3 us -> 12.1 us  [per_device(): kv_rows = lax.all_gather(kv_part, 'z', axis=0, tiled=True)]
    all_to_all x1, blocking collectives: 38.5 us -> 34.8 us  [per_device(): lax.all_to_all(produced.reshape(group_count, rows, HD), group, split_axis...]
  transfers between devices with their start and end apart: 2 -> 1, of which waited for: 1 -> 1; matrix products, arithmetic and copies ran while one was open for 5% -> 5% of each run, Pallas kernels for 9% -> 0%
where the time goes in v7:
time: 156 us; the launch traced here: 155 us
  blocking collectives  88.9 us (57%)
  Pallas kernels  29 us (19%)
  between operations  13.5 us (9%)
  waiting for transfers between devices  12.1 us (8%)
  local copies, waits for them, and re-layouts  10.6 us (7%)
    all_to_all x1, blocking collectives, per_device(): lax.all_to_all(produced.reshape(group_count, rows, HD), group, split_axis...  34.8 us
    all_to_all x1, blocking collectives, per_device(): lax.all_to_all(q_heads, group, split_axis=0, concat_axis=0, tiled=True)  34.2 us
    all_to_all x1, blocking collectives, per_device(): lax.all_to_all(kv_heads, group, split_axis=0, concat_axis=0, tiled=True)  19.9 us
    pallas_call x1, Pallas kernels, attend(): pl.pallas_call(functools.partial(weights_kernel, per_step=per_step, per_d...  16.5 us
    pallas_call x1, Pallas kernels, attend(): pl.pallas_call(functools.partial(mix_kernel, per_step=per_step), grid_spe...  12.5 us
    all_gather x1, waiting for transfers between devices, per_device(): kv_rows = lax.all_gather(kv_part, 'z', axis=0, tiled=True)  12.1 us
    unnamed x13, local copies, waits for them, and re-layouts  3.36 us
    reshape x1, local copies, waits for them, and re-layouts, per_device(): queries.reshape(rows, HEADS, HD).transpose(1, 0, 2)  3.21 us
  transfers between devices with their start and end apart: 1, of which 1 were waited for; matrix products, arithmetic and copies ran while one was open for 5% of the time, Pallas kernels for 0%

profile of v7, /device:TPU:1, one launch (start us, length us, event | category | flops | bytes accessed | tf_op | source)
XLA Modules:
  0.0 155.3 jit_solution(9029364623503043833)
XLA Ops:
  6.5 0.0 copy-start
  6.5 0.0 all-gather.2.cloned.1.call-start
  6.6 0.9 copy-done
  7.5 1.0 bitcast_bitcast_fusion
  8.5 0.1 pad_maximum_fusion.1
  8.6 19.9 %all_to_all.15 = bf16[32,32,256]{2,1,0:T(8,128)(2,1)} all-to-all(bf16[32,32,256]{2,1,0:T(8,128)(2,1)S(1)} %pad_maximum_fusion.1), channel_id=1, replica_groups=mesh['y'=4,'core'=2,'z'=8,'x'=4] {'y','core','x'}, dimensions={0} | all-to-all | bytes 1048576 | tf_op jit(solution)/shard_map/all_to_all | solution.py:143
  28.5 0.0 all-gather.2.cloned.1.call-update
  28.5 0.0 copy-done.5
  28.5 0.1 convert_bitcast_fusion
  28.6 0.0 copy-done.4
  28.6 0.1 dynamic-slice_convert_fusion
  28.7 0.1 copy.19
  28.8 0.1 convert_element_type.22
  28.9 0.0 copy-done.2
  28.9 2.4 %copy.17 = bf16[256,4096]{0,1:T(8,128)(2,1)} copy(bf16[256,4096]{1,0:T(8,128)(2,1)S(1)} %copy-done.2) | data formatting | bytes 4194304 | tf_op args[0]
  31.3 3.2 %copy.18 = bf16[256,32,128]{2,0,1:T(8,128)(2,1)S(1)} copy(bf16[256,32,128]{0,2,1:T(8,128)(2,1)} %bitcast.27) | data formatting | bytes 4194304 | tf_op jit(solution)/shard_map/reshape | solution.py:156
  34.6 0.2 pad_maximum_fusion
  34.8 34.2 %all_to_all.16.q_ref = bf16[32,272,128]{2,1,0:T(8,128)(2,1)S(1)} all-to-all(bf16[32,272,128]{2,1,0:T(8,128)(2,1)S(1)} %pad_maximum_fusion), channel_id=1, replica_groups=mesh['y'=4,'core'=2,'z'=8,'x'=4] {'y','core','x'}, dimensions={0} | all-to-all | bytes 4456448 | tf_op jit(solution)/shard_map/all_to_all | solution.py:161
  69.0 0.1 fusion.6
  69.1 0.1 reshape.75
  69.2 0.8 reshape.69.lists_ref
  70.0 0.2 slice_reduce_fusion.counts_ref
  70.2 0.0 copy-start.3
  70.2 0.1 reshape_squeeze.3
  70.3 0.1 reduce_max.9
  70.4 0.5 fusion.7.step_ref
  70.9 12.1 %all-gather.2.cloned.1.call-done.k_ref.v_ref = bf16[8192,256]{1,0:T(8,128)(2,1)} async-done(((bf16[1024,256]{1,0:T(8,128)(2,1)}), bf16[8192,256]{1,0:T(8,128)(2,1)}) %all-gather.2.cloned.1.call-update) | async-done | bytes 4194320 | tf_op jit(solution)/shard_map/all_gather | solution.py:145
  83.0 0.0 copy-done.3
  83.0 16.5 %shard_map.55.w_ref = bf16[64,128,1024]{2,1,0:T(8,128)(2,1)} custom-call(s32[8]{0:T(128)} %fusion.7.step_ref, s32[512]{0:T(512)} %reshape.69.lists_ref, s32[64]{0:T(128)} %copy-done.3, bf16[32,272,128]{2,1,0:T(8,128)(2,1)} %copy-done.1, bf16[8192,256]{1,0:T(8,128)(2,1)} %all-gather.2.cloned.1.call-done.k_ref.v_ref), custom_call_target="tpu_custom_call" | custom-call | flops 2147483648 | bytes 20971520 | tf_op jit(solution)/shard_map/pallas_call | solution.py:78
  99.6 12.5 %shard_map.56 = bf16[64,128,128]{2,1,0:T(8,128)(2,1)} custom-call(s32[8]{0:T(128)} %fusion.7.step_ref, s32[512]{0:T(512)} %reshape.69.lists_ref, bf16[64,128,1024]{2,1,0:T(8,128)(2,1)} %shard_map.55.w_ref, bf16[8192,256]{1,0:T(8,128)(2,1)} %all-gather.2.cloned.1.call-done.k_ref.v_ref), custom_call_target="tpu_custom_call" | custom-call | flops 2147483648 | bytes 20971520 | tf_op jit(solution)/shard_map/pallas_call | solution.py:99
  112.1 34.8 %all_to_all.17 = bf16[32,256,128]{2,1,0:T(8,128)(2,1)S(1)} all-to-all(bf16[32,256,128]{2,1,0:T(8,128)(2,1)} %bitcast.28), channel_id=1, replica_groups=mesh['y'=4,'core'=2,'z'=8,'x'=4] {'y','core','x'}, dimensions={0} | all-to-all | bytes 4194304 | tf_op jit(solution)/shard_map/all_to_all | solution.py:170
  146.9 1.6 %copy_bitcast_fusion = bf16[256,4096]{1,0:T(8,128)(2,1)} fusion(bf16[32,256,128]{2,1,0:T(8,128)(2,1)S(1)} %all_to_all.17), kind=kLoop, calls=%fused_computation.1 | loop fusion | bytes 4194304 | tf_op jit(solution)/shard_map/reshape | solution.py:173
  (9 shorter events, 0.1 us)
Async XLA Ops:
  6.5 1.0 copy-start
  6.5 22.0 %copy-start.5 = (s32[64]{0:T(128)S(1)}, s32[64]{0:T(128)}, u32[]{:S(2)}) copy-start(s32[64]{0:T(128)} %param.11) | copy-start | bytes 772
  6.5 22.1 %copy-start.4 = (s32[64,8]{0,1:T(8,128)S(1)}, s32[64,8]{0,1:T(8,128)}, u32[]{:S(2)}) copy-start(s32[64,8]{0,1:T(8,128)} %param.10) | copy-start | bytes 6148
  6.5 22.4 %copy-start.2 = (bf16[256,4096]{1,0:T(8,128)(2,1)S(1)}, bf16[256,4096]{1,0:T(8,128)(2,1)}, u32[]{:S(2)}) copy-start(bf16[256,4096]{1,0:T(8,128)(2,1)} %param.7) | copy-start | bytes 6291460
  6.5 76.5 %all-gather.2.cloned.1.call-start = ((), (), s32[]{:S(2)}) async-start(), calls=%async_computation.3 | async-start | bytes 4718592 | tf_op jit(solution)/shard_map/all_gather | solution.py:145
  69.0 14.0 %copy-start.1 = (bf16[32,272,128]{2,1,0:T(8,128)(2,1)}, bf16[32,272,128]{2,1,0:T(8,128)(2,1)S(1)}, u32[]{:S(2)}) copy-start(bf16[32,272,128]{2,1,0:T(8,128)(2,1)S(1)} %all_to_all.16.q_ref) | copy-start | bytes 6684676
  70.2 12.9 %copy-start.3 = (s32[64]{0:T(128)}, s32[64]{0:T(128)S(1)}, u32[]{:S(2)}) copy-start(s32[64]{0:T(128)S(1)} %slice_reduce_fusion.counts_ref) | copy-start | bytes 772
Sparse Core Ops, SparseCore 0:
  28.6 54.3 all-gather.1

commit v8 on v7

--- a/solution.py
+++ b/solution.py
@@ -13,7 +13,7 @@
 MOST = 8
 
 
-SLOT_SIZES = (2, 4, MOST)
+SLOT_SIZES = (2, 4, 6, MOST)
 
 
 def weights_kernel(step_ref, lists_ref, counts_ref, q_ref, k_ref, w_ref, kc_ref,

time: 156 us -> 153 us (0.981)
  Pallas kernels: 29 us -> 26.2 us
    pallas_call x1, Pallas kernels: 16.5 us -> 14.2 us  [attend(): pl.pallas_call(functools.partial(weights_kernel, per_step=per_step, per_d...]
where the time goes in v8:
time: 153 us; the launch traced here: 152 us
  blocking collectives  88.9 us (58%)
  Pallas kernels  26.2 us (17%)
  between operations  13.5 us (9%)
  waiting for transfers between devices  12.1 us (8%)
  local copies, waits for them, and re-layouts  10.6 us (7%)
    all_to_all x1, blocking collectives, per_device(): lax.all_to_all(produced.reshape(group_count, rows, HD), group, split_axis...  34.8 us
    all_to_all x1, blocking collectives, per_device(): lax.all_to_all(q_heads, group, split_axis=0, concat_axis=0, tiled=True)  34.2 us
    all_to_all x1, blocking collectives, per_device(): lax.all_to_all(kv_heads, group, split_axis=0, concat_axis=0, tiled=True)  19.9 us
    pallas_call x1, Pallas kernels, attend(): pl.pallas_call(functools.partial(weights_kernel, per_step=per_step, per_d...  14.2 us
    all_gather x1, waiting for transfers between devices, per_device(): kv_rows = lax.all_gather(kv_part, 'z', axis=0, tiled=True)  12.1 us
    pallas_call x1, Pallas kernels, attend(): pl.pallas_call(functools.partial(mix_kernel, per_step=per_step), grid_spe...  12 us
    unnamed x13, local copies, waits for them, and re-layouts  3.36 us
    reshape x1, local copies, waits for them, and re-layouts, per_device(): queries.reshape(rows, HEADS, HD).transpose(1, 0, 2)  3.21 us
  transfers between devices with their start and end apart: 1, of which 1 were waited for; matrix products, arithmetic and copies ran while one was open for 5% of the time, Pallas kernels for 0%

profile of v8, /device:TPU:1, one launch (start us, length us, event | category | flops | bytes accessed | tf_op | source)
XLA Modules:
  0.0 152.5 jit_solution(7015464560585963090)
XLA Ops:
  6.5 0.0 copy-start
  6.5 0.0 all-gather.2.cloned.1.call-start
  6.6 0.9 copy-done
  7.5 1.0 bitcast_bitcast_fusion
  8.5 0.1 pad_maximum_fusion.1
  8.6 19.9 %all_to_all.15 = bf16[32,32,256]{2,1,0:T(8,128)(2,1)} all-to-all(bf16[32,32,256]{2,1,0:T(8,128)(2,1)S(1)} %pad_maximum_fusion.1), channel_id=1, replica_groups=mesh['y'=4,'core'=2,'z'=8,'x'=4] {'y','core','x'}, dimensions={0} | all-to-all | bytes 1048576 | tf_op jit(solution)/shard_map/all_to_all | solution.py:143
  28.5 0.0 all-gather.2.cloned.1.call-update
  28.5 0.0 copy-done.5
  28.5 0.1 convert_bitcast_fusion
  28.6 0.0 copy-done.4
  28.6 0.1 dynamic-slice_convert_fusion
  28.7 0.1 copy.19
  28.8 0.1 convert_element_type.25
  28.9 0.0 copy-done.2
  28.9 2.4 %copy.17 = bf16[256,4096]{0,1:T(8,128)(2,1)} copy(bf16[256,4096]{1,0:T(8,128)(2,1)S(1)} %copy-done.2) | data formatting | bytes 4194304 | tf_op args[0]
  31.3 3.2 %copy.18 = bf16[256,32,128]{2,0,1:T(8,128)(2,1)S(1)} copy(bf16[256,32,128]{0,2,1:T(8,128)(2,1)} %bitcast.27) | data formatting | bytes 4194304 | tf_op jit(solution)/shard_map/reshape | solution.py:156
  34.6 0.2 pad_maximum_fusion
  34.8 34.2 %all_to_all.16.q_ref = bf16[32,272,128]{2,1,0:T(8,128)(2,1)S(1)} all-to-all(bf16[32,272,128]{2,1,0:T(8,128)(2,1)S(1)} %pad_maximum_fusion), channel_id=1, replica_groups=mesh['y'=4,'core'=2,'z'=8,'x'=4] {'y','core','x'}, dimensions={0} | all-to-all | bytes 4456448 | tf_op jit(solution)/shard_map/all_to_all | solution.py:161
  69.0 0.1 fusion.6
  69.1 0.1 reshape.75
  69.2 0.8 reshape.69.lists_ref
  70.0 0.2 slice_reduce_fusion.counts_ref
  70.2 0.0 copy-start.3
  70.2 0.1 reshape_squeeze.3
  70.3 0.1 reduce_max.9
  70.4 0.5 fusion.8.step_ref
  70.9 12.1 %all-gather.2.cloned.1.call-done.k_ref.v_ref = bf16[8192,256]{1,0:T(8,128)(2,1)} async-done(((bf16[1024,256]{1,0:T(8,128)(2,1)}), bf16[8192,256]{1,0:T(8,128)(2,1)}) %all-gather.2.cloned.1.call-update) | async-done | bytes 4194320 | tf_op jit(solution)/shard_map/all_gather | solution.py:145
  83.0 0.0 copy-done.1
  83.0 14.2 %shard_map.55.w_ref = bf16[64,128,1024]{2,1,0:T(8,128)(2,1)} custom-call(s32[8]{0:T(128)} %fusion.8.step_ref, s32[512]{0:T(512)} %reshape.69.lists_ref, s32[64]{0:T(128)} %copy-done.3, bf16[32,272,128]{2,1,0:T(8,128)(2,1)} %copy-done.1, bf16[8192,256]{1,0:T(8,128)(2,1)} %all-gather.2.cloned.1.call-done.k_ref.v_ref), custom_call_target="tpu_custom_call" | custom-call | flops 2147483648 | bytes 20971520 | tf_op jit(solution)/shard_map/pallas_call | solution.py:78
  97.2 12.0 %shard_map.56 = bf16[64,128,128]{2,1,0:T(8,128)(2,1)} custom-call(s32[8]{0:T(128)} %fusion.8.step_ref, s32[512]{0:T(512)} %reshape.69.lists_ref, bf16[64,128,1024]{2,1,0:T(8,128)(2,1)} %shard_map.55.w_ref, bf16[8192,256]{1,0:T(8,128)(2,1)} %all-gather.2.cloned.1.call-done.k_ref.v_ref), custom_call_target="tpu_custom_call" | custom-call | flops 2147483648 | bytes 20971520 | tf_op jit(solution)/shard_map/pallas_call | solution.py:99
  109.2 34.8 %all_to_all.17 = bf16[32,256,128]{2,1,0:T(8,128)(2,1)S(1)} all-to-all(bf16[32,256,128]{2,1,0:T(8,128)(2,1)} %bitcast.28), channel_id=1, replica_groups=mesh['y'=4,'core'=2,'z'=8,'x'=4] {'y','core','x'}, dimensions={0} | all-to-all | bytes 4194304 | tf_op jit(solution)/shard_map/all_to_all | solution.py:170
  144.0 1.6 %copy_bitcast_fusion = bf16[256,4096]{1,0:T(8,128)(2,1)} fusion(bf16[32,256,128]{2,1,0:T(8,128)(2,1)S(1)} %all_to_all.17), kind=kLoop, calls=%fused_computation.1 | loop fusion | bytes 4194304 | tf_op jit(solution)/shard_map/reshape | solution.py:173
  (9 shorter events, 0.1 us)
Async XLA Ops:
  6.5 1.0 copy-start
  6.5 22.0 %copy-start.5 = (s32[64]{0:T(128)S(1)}, s32[64]{0:T(128)}, u32[]{:S(2)}) copy-start(s32[64]{0:T(128)} %param.11) | copy-start | bytes 772
  6.5 22.1 %copy-start.4 = (s32[64,8]{0,1:T(8,128)S(1)}, s32[64,8]{0,1:T(8,128)}, u32[]{:S(2)}) copy-start(s32[64,8]{0,1:T(8,128)} %param.10) | copy-start | bytes 6148
  6.5 22.4 %copy-start.2 = (bf16[256,4096]{1,0:T(8,128)(2,1)S(1)}, bf16[256,4096]{1,0:T(8,128)(2,1)}, u32[]{:S(2)}) copy-start(bf16[256,4096]{1,0:T(8,128)(2,1)} %param.7) | copy-start | bytes 6291460
  6.5 76.5 %all-gather.2.cloned.1.call-start = ((), (), s32[]{:S(2)}) async-start(), calls=%async_computation.3 | async-start | bytes 4718592 | tf_op jit(solution)/shard_map/all_gather | solution.py:145
  69.0 14.0 %copy-start.1 = (bf16[32,272,128]{2,1,0:T(8,128)(2,1)}, bf16[32,272,128]{2,1,0:T(8,128)(2,1)S(1)}, u32[]{:S(2)}) copy-start(bf16[32,272,128]{2,1,0:T(8,128)(2,1)S(1)} %all_to_all.16.q_ref) | copy-start | bytes 6684676
  70.2 12.9 %copy-start.3 = (s32[64]{0:T(128)}, s32[64]{0:T(128)S(1)}, u32[]{:S(2)}) copy-start(s32[64]{0:T(128)S(1)} %slice_reduce_fusion.counts_ref) | copy-start | bytes 772
Sparse Core Ops, SparseCore 0:
  28.6 54.3 all-gather.1

commit v9 on v8

--- a/solution.py
+++ b/solution.py
@@ -13,7 +13,7 @@
 MOST = 8
 
 
-SLOT_SIZES = (2, 4, 6, MOST)
+SLOT_SIZES = (2, 3, 4, 5, 6, 7, MOST)
 
 
 def weights_kernel(step_ref, lists_ref, counts_ref, q_ref, k_ref, w_ref, kc_ref,

time: 153 us -> 152 us (level)
  Pallas kernels: 26.2 us -> 24.5 us
    pallas_call x1, Pallas kernels: 14.2 us -> 12.6 us  [attend(): pl.pallas_call(functools.partial(weights_kernel, per_step=per_step, per_d...]
where the time goes in v9:
time: 152 us; the launch traced here: 151 us
  blocking collectives  88.9 us (58%)
  Pallas kernels  24.5 us (16%)
  between operations  13.5 us (9%)
  waiting for transfers between devices  12.1 us (8%)
  local copies, waits for them, and re-layouts  10.6 us (7%)
    all_to_all x1, blocking collectives, per_device(): lax.all_to_all(produced.reshape(group_count, rows, HD), group, split_axis...  34.8 us
    all_to_all x1, blocking collectives, per_device(): lax.all_to_all(q_heads, group, split_axis=0, concat_axis=0, tiled=True)  34.2 us
    all_to_all x1, blocking collectives, per_device(): lax.all_to_all(kv_heads, group, split_axis=0, concat_axis=0, tiled=True)  19.9 us
    pallas_call x1, Pallas kernels, attend(): pl.pallas_call(functools.partial(weights_kernel, per_step=per_step, per_d...  12.6 us
    all_gather x1, waiting for transfers between devices, per_device(): kv_rows = lax.all_gather(kv_part, 'z', axis=0, tiled=True)  12.1 us
    pallas_call x1, Pallas kernels, attend(): pl.pallas_call(functools.partial(mix_kernel, per_step=per_step), grid_spe...  11.9 us
    unnamed x13, local copies, waits for them, and re-layouts  3.36 us
    reshape x1, local copies, waits for them, and re-layouts, per_device(): queries.reshape(rows, HEADS, HD).transpose(1, 0, 2)  3.21 us
  transfers between devices with their start and end apart: 1, of which 1 were waited for; matrix products, arithmetic and copies ran while one was open for 5% of the time, Pallas kernels for 0%

profile of v9, /device:TPU:1, one launch (start us, length us, event | category | flops | bytes accessed | tf_op | source)
XLA Modules:
  0.0 150.8 jit_solution(7519234543917693215)
XLA Ops:
  6.5 0.0 copy-start
  6.5 0.0 all-gather.2.cloned.1.call-start
  6.6 0.9 copy-done
  7.5 1.0 bitcast_bitcast_fusion
  8.5 0.1 pad_maximum_fusion.1
  8.6 19.9 %all_to_all.15 = bf16[32,32,256]{2,1,0:T(8,128)(2,1)} all-to-all(bf16[32,32,256]{2,1,0:T(8,128)(2,1)S(1)} %pad_maximum_fusion.1), channel_id=1, replica_groups=mesh['y'=4,'core'=2,'z'=8,'x'=4] {'y','core','x'}, dimensions={0} | all-to-all | bytes 1048576 | tf_op jit(solution)/shard_map/all_to_all | solution.py:143
  28.5 0.0 all-gather.2.cloned.1.call-update
  28.5 0.0 copy-done.5
  28.5 0.1 convert_bitcast_fusion
  28.6 0.0 copy-done.4
  28.6 0.1 dynamic-slice_convert_fusion
  28.7 0.1 copy.19
  28.8 0.1 convert_element_type.34
  28.9 0.0 copy-done.2
  28.9 2.4 %copy.17 = bf16[256,4096]{0,1:T(8,128)(2,1)} copy(bf16[256,4096]{1,0:T(8,128)(2,1)S(1)} %copy-done.2) | data formatting | bytes 4194304 | tf_op args[0]
  31.3 3.2 %copy.18 = bf16[256,32,128]{2,0,1:T(8,128)(2,1)S(1)} copy(bf16[256,32,128]{0,2,1:T(8,128)(2,1)} %bitcast.27) | data formatting | bytes 4194304 | tf_op jit(solution)/shard_map/reshape | solution.py:156
  34.6 0.2 pad_maximum_fusion
  34.8 34.2 %all_to_all.16.q_ref = bf16[32,272,128]{2,1,0:T(8,128)(2,1)S(1)} all-to-all(bf16[32,272,128]{2,1,0:T(8,128)(2,1)S(1)} %pad_maximum_fusion), channel_id=1, replica_groups=mesh['y'=4,'core'=2,'z'=8,'x'=4] {'y','core','x'}, dimensions={0} | all-to-all | bytes 4456448 | tf_op jit(solution)/shard_map/all_to_all | solution.py:161
  69.0 0.1 fusion.6
  69.1 0.1 reshape.75
  69.2 0.8 reshape.69.lists_ref
  70.0 0.2 slice_reduce_fusion.counts_ref
  70.2 0.0 copy-start.3
  70.2 0.1 reshape_squeeze.3
  70.3 0.1 reduce_max.9
  70.4 0.5 fusion.11.step_ref
  70.9 12.1 %all-gather.2.cloned.1.call-done.k_ref.v_ref = bf16[8192,256]{1,0:T(8,128)(2,1)} async-done(((bf16[1024,256]{1,0:T(8,128)(2,1)}), bf16[8192,256]{1,0:T(8,128)(2,1)}) %all-gather.2.cloned.1.call-update) | async-done | bytes 4194320 | tf_op jit(solution)/shard_map/all_gather | solution.py:145
  83.0 0.0 copy-done.3
  83.0 12.6 %shard_map.55.w_ref = bf16[64,128,1024]{2,1,0:T(8,128)(2,1)} custom-call(s32[8]{0:T(128)} %fusion.11.step_ref, s32[512]{0:T(512)} %reshape.69.lists_ref, s32[64]{0:T(128)} %copy-done.3, bf16[32,272,128]{2,1,0:T(8,128)(2,1)} %copy-done.1, bf16[8192,256]{1,0:T(8,128)(2,1)} %all-gather.2.cloned.1.call-done.k_ref.v_ref), custom_call_target="tpu_custom_call" | custom-call | flops 2147483648 | bytes 20971520 | tf_op jit(solution)/shard_map/pallas_call | solution.py:78
  95.7 11.9 %shard_map.56 = bf16[64,128,128]{2,1,0:T(8,128)(2,1)} custom-call(s32[8]{0:T(128)} %fusion.11.step_ref, s32[512]{0:T(512)} %reshape.69.lists_ref, bf16[64,128,1024]{2,1,0:T(8,128)(2,1)} %shard_map.55.w_ref, bf16[8192,256]{1,0:T(8,128)(2,1)} %all-gather.2.cloned.1.call-done.k_ref.v_ref), custom_call_target="tpu_custom_call" | custom-call | flops 2147483648 | bytes 20971520 | tf_op jit(solution)/shard_map/pallas_call | solution.py:99
  107.6 34.8 %all_to_all.17 = bf16[32,256,128]{2,1,0:T(8,128)(2,1)S(1)} all-to-all(bf16[32,256,128]{2,1,0:T(8,128)(2,1)} %bitcast.28), channel_id=1, replica_groups=mesh['y'=4,'core'=2,'z'=8,'x'=4] {'y','core','x'}, dimensions={0} | all-to-all | bytes 4194304 | tf_op jit(solution)/shard_map/all_to_all | solution.py:170
  142.3 1.6 %copy_bitcast_fusion = bf16[256,4096]{1,0:T(8,128)(2,1)} fusion(bf16[32,256,128]{2,1,0:T(8,128)(2,1)S(1)} %all_to_all.17), kind=kLoop, calls=%fused_computation.1 | loop fusion | bytes 4194304 | tf_op jit(solution)/shard_map/reshape | solution.py:173
  (9 shorter events, 0.1 us)
Async XLA Ops:
  6.5 1.0 copy-start
  6.5 22.0 %copy-start.5 = (s32[64]{0:T(128)S(1)}, s32[64]{0:T(128)}, u32[]{:S(2)}) copy-start(s32[64]{0:T(128)} %param.11) | copy-start | bytes 772
  6.5 22.1 %copy-start.4 = (s32[64,8]{0,1:T(8,128)S(1)}, s32[64,8]{0,1:T(8,128)}, u32[]{:S(2)}) copy-start(s32[64,8]{0,1:T(8,128)} %param.10) | copy-start | bytes 6148
  6.5 22.4 %copy-start.2 = (bf16[256,4096]{1,0:T(8,128)(2,1)S(1)}, bf16[256,4096]{1,0:T(8,128)(2,1)}, u32[]{:S(2)}) copy-start(bf16[256,4096]{1,0:T(8,128)(2,1)} %param.7) | copy-start | bytes 6291460
  6.5 76.5 %all-gather.2.cloned.1.call-start = ((), (), s32[]{:S(2)}) async-start(), calls=%async_computation.3 | async-start | bytes 4718592 | tf_op jit(solution)/shard_map/all_gather | solution.py:145
  69.0 14.0 %copy-start.1 = (bf16[32,272,128]{2,1,0:T(8,128)(2,1)}, bf16[32,272,128]{2,1,0:T(8,128)(2,1)S(1)}, u32[]{:S(2)}) copy-start(bf16[32,272,128]{2,1,0:T(8,128)(2,1)S(1)} %all_to_all.16.q_ref) | copy-start | bytes 6684676
  70.2 12.9 %copy-start.3 = (s32[64]{0:T(128)}, s32[64]{0:T(128)S(1)}, u32[]{:S(2)}) copy-start(s32[64]{0:T(128)S(1)} %slice_reduce_fusion.counts_ref) | copy-start | bytes 772
Sparse Core Ops, SparseCore 0:
  28.6 54.3 all-gather.1

commit v10 on v9

--- a/solution.py
+++ b/solution.py
@@ -14,9 +14,10 @@
 
 
 SLOT_SIZES = (2, 3, 4, 5, 6, 7, MOST)
-
-
-def weights_kernel(step_ref, lists_ref, counts_ref, q_ref, k_ref, w_ref, kc_ref,
+HALF = MOST // 2
+
+
+def weights_kernel(step_ref, hi_ref, lists_ref, counts_ref, q_ref, k_ref, wlo_ref, whi_ref, kc_ref,
                    *, per_step, per_dev, scaling):
     step = pl.program_id(0)
 
@@ -37,13 +38,17 @@
                 m = jnp.max(sc, axis=-1, keepdims=True)
                 p = jnp.exp(sc - m)
                 l = jnp.sum(p, axis=-1, keepdims=True)
-                w_ref[i, :, pl.ds(0, slots * BLK)] = (p / l).astype(jnp.bfloat16)
+                w = (p / l).astype(jnp.bfloat16)
+                low = min(slots, HALF) * BLK
+                wlo_ref[i, :, pl.ds(0, low)] = w[:, :low]
+                if slots > HALF:
+                    whi_ref[i, :, pl.ds(0, slots * BLK - low)] = w[:, low:]
         return body
 
     lax.switch(step_ref[step], [body_for(n) for n in SLOT_SIZES])
 
 
-def mix_kernel(step_ref, lists_ref, w_ref, v_ref, o_ref, vc_ref, *, per_step):
+def mix_kernel(step_ref, hi_ref, lists_ref, wlo_ref, whi_ref, v_ref, o_ref, vc_ref, *, per_step):
     step = pl.program_id(0)
 
     def body_for(slots):
@@ -54,9 +59,13 @@
                     kb = lists_ref[qb * MOST + s]
                     start = pl.multiple_of(kb * BLK, BLK)
                     vc_ref[pl.ds(s * BLK, BLK), :] = v_ref[pl.ds(start, BLK), :]
-                w = w_ref[i, :, pl.ds(0, slots * BLK)]
-                out = jnp.dot(w, vc_ref[pl.ds(0, slots * BLK), :],
+                low = min(slots, HALF) * BLK
+                out = jnp.dot(wlo_ref[i, :, pl.ds(0, low)], vc_ref[pl.ds(0, low), :],
                               preferred_element_type=jnp.float32)
+                if slots > HALF:
+                    out = out + jnp.dot(whi_ref[i, :, pl.ds(0, slots * BLK - low)],
+                                        vc_ref[pl.ds(low, slots * BLK - low), :],
+                                        preferred_element_type=jnp.float32)
                 o_ref[i] = out.astype(o_ref.dtype)
         return body
 
@@ -69,44 +78,51 @@
     per_src = 4 if sources % 4 == 0 else 1
     per_step = per_src * per_dev
     nk = kv_rows.shape[0]
-    width = MOST * BLK
+    width = HALF * BLK
     widest = jnp.max(counts.reshape(blocks // per_step, per_step), axis=1)
     step_size = jnp.zeros_like(widest)
     for n in SLOT_SIZES[:-1]:
         step_size = step_size + (widest > n).astype(jnp.int32)
     flat_lists = lists.reshape(-1)
+    steps = blocks // per_step
+    big = widest > HALF
+    hi_index = lax.cummax(jnp.where(big, jnp.arange(steps, dtype=jnp.int32), 0))
     weights = pl.pallas_call(
         functools.partial(weights_kernel, per_step=per_step, per_dev=per_dev,
                           scaling=HD ** (-0.5)),
         grid_spec=pltpu.PrefetchScalarGridSpec(
-            num_scalar_prefetch=3,
+            num_scalar_prefetch=4,
             grid=(blocks // per_step,),
             in_specs=[
                 pl.BlockSpec((per_src, per_dev * BLK, HD), lambda b, *_: (b, 0, 0)),
                 pl.BlockSpec((nk, HD), lambda b, *_: (0, 0)),
             ],
-            out_specs=pl.BlockSpec((per_step, BLK, width), lambda b, *_: (b, 0, 0)),
-            scratch_shapes=[pltpu.VMEM((width, HD), jnp.bfloat16)],
-        ),
-        out_shape=jax.ShapeDtypeStruct((blocks, BLK, width), jnp.bfloat16),
+            out_specs=[
+                pl.BlockSpec((per_step, BLK, width), lambda b, *_: (b, 0, 0)),
+                pl.BlockSpec((per_step, BLK, width), lambda b, s, h, *_: (h[b], 0, 0)),
+            ],
+            scratch_shapes=[pltpu.VMEM((MOST * BLK, HD), jnp.bfloat16)],
+        ),
+        out_shape=[jax.ShapeDtypeStruct((blocks, BLK, width), jnp.bfloat16)] * 2,
         compiler_params=pltpu.CompilerParams(dimension_semantics=("arbitrary",)),
         cost_estimate=pl.CostEstimate(
             flops=blocks * 2 * BLK * width * HD,
             transcendentals=blocks * BLK * width,
             bytes_accessed=kv_rows.size + blocks * BLK * (HD + width) * 2,
         ),
-    )(step_size, flat_lists, counts, q_src, kv_rows)
+    )(step_size, hi_index, flat_lists, counts, q_src, kv_rows)
     return pl.pallas_call(
         functools.partial(mix_kernel, per_step=per_step),
         grid_spec=pltpu.PrefetchScalarGridSpec(
-            num_scalar_prefetch=2,
+            num_scalar_prefetch=3,
             grid=(blocks // per_step,),
             in_specs=[
                 pl.BlockSpec((per_step, BLK, width), lambda b, *_: (b, 0, 0)),
+                pl.BlockSpec((per_step, BLK, width), lambda b, s, h, *_: (h[b], 0, 0)),
                 pl.BlockSpec((nk, HD), lambda b, *_: (0, 1)),
             ],
             out_specs=pl.BlockSpec((per_step, BLK, HD), lambda b, *_: (b, 0, 0)),
-            scratch_shapes=[pltpu.VMEM((width, HD), jnp.bfloat16)],
+            scratch_shapes=[pltpu.VMEM((MOST * BLK, HD), jnp.bfloat16)],
         ),
         out_shape=jax.ShapeDtypeStruct((blocks, BLK, HD), jnp.bfloat16),
         compiler_params=pltpu.CompilerParams(dimension_semantics=("arbitrary",)),
@@ -115,7 +131,7 @@
             transcendentals=0,
             bytes_accessed=kv_rows.size + blocks * BLK * (HD + width) * 2,
         ),
-    )(step_size, flat_lists, weights, kv_rows)
+    )(step_size, hi_index, flat_lists, weights[0], weights[1], kv_rows)
 
 
 def per_device(queries, keys, values, key_lists, counts, *, x_count):

time: 152 us -> 153 us (level); the launches traced: 151 us -> 154 us
  Pallas kernels: 24.5 us -> 27.4 us
    pallas_call x1, Pallas kernels: 12.6 us -> 15.4 us  [attend(): pl.pallas_call(functools.partial(weights_kernel, per_step=per_step, per_d...]
  transfers between devices with their start and end apart: 1 -> 1, of which waited for: 1 -> 1; matrix products, arithmetic and copies ran while one was open for 5% -> 6% of each run, Pallas kernels for 0% -> 0%
where the time goes in v10:
time: 153 us; the launch traced here: 154 us
  blocking collectives  88.9 us (58%)
  Pallas kernels  27.4 us (18%)
  between operations  13.5 us (9%)
  waiting for transfers between devices  11.4 us (7%)
  local copies, waits for them, and re-layouts  10.7 us (7%)
  other arithmetic  1.83 us (1%)
    all_to_all x1, blocking collectives, per_device(): lax.all_to_all(produced.reshape(group_count, rows, HD), group, split_axis...  34.8 us
    all_to_all x1, blocking collectives, per_device(): lax.all_to_all(q_heads, group, split_axis=0, concat_axis=0, tiled=True)  34.2 us
    all_to_all x1, blocking collectives, per_device(): lax.all_to_all(kv_heads, group, split_axis=0, concat_axis=0, tiled=True)  19.9 us
    pallas_call x1, Pallas kernels, attend(): pl.pallas_call(functools.partial(weights_kernel, per_step=per_step, per_d...  15.4 us
    pallas_call x1, Pallas kernels, attend(): pl.pallas_call(functools.partial(mix_kernel, per_step=per_step), grid_spe...  12 us
    all_gather x1, waiting for transfers between devices, per_device(): kv_rows = lax.all_gather(kv_part, 'z', axis=0, tiled=True)  11.4 us
    unnamed x13, local copies, waits for them, and re-layouts  3.36 us
    reshape x1, local copies, waits for them, and re-layouts, per_device(): queries.reshape(rows, HEADS, HD).transpose(1, 0, 2)  3.21 us
  transfers between devices with their start and end apart: 1, of which 1 were waited for; matrix products, arithmetic and copies ran while one was open for 6% of the time, Pallas kernels for 0%

profile of v10, /device:TPU:1, one launch (start us, length us, event | category | flops | bytes accessed | tf_op | source)
XLA Modules:
  0.0 153.7 jit_solution(8071652362468507936)
XLA Ops:
  6.5 0.0 copy-start
  6.5 0.0 all-gather.2.cloned.1.call-start
  6.6 0.9 copy-done
  7.5 1.0 bitcast_bitcast_fusion
  8.5 0.1 pad_maximum_fusion.1
  8.6 19.9 %all_to_all.15 = bf16[32,32,256]{2,1,0:T(8,128)(2,1)} all-to-all(bf16[32,32,256]{2,1,0:T(8,128)(2,1)S(1)} %pad_maximum_fusion.1), channel_id=1, replica_groups=mesh['y'=4,'core'=2,'z'=8,'x'=4] {'y','core','x'}, dimensions={0} | all-to-all | bytes 1048576 | tf_op jit(solution)/shard_map/all_to_all | solution.py:159
  28.5 0.0 all-gather.2.cloned.1.call-update
  28.5 0.0 copy-done.5
  28.5 0.1 convert_bitcast_fusion
  28.6 0.0 copy-done.3
  28.6 0.1 dynamic-slice_convert_fusion
  28.7 0.1 copy.19
  28.8 0.1 convert_element_type.34
  28.9 0.0 copy-done.2
  28.9 2.4 %copy.17 = bf16[256,4096]{0,1:T(8,128)(2,1)} copy(bf16[256,4096]{1,0:T(8,128)(2,1)S(1)} %copy-done.2) | data formatting | bytes 4194304 | tf_op args[0]
  31.3 3.2 %copy.18 = bf16[256,32,128]{2,0,1:T(8,128)(2,1)S(1)} copy(bf16[256,32,128]{0,2,1:T(8,128)(2,1)} %bitcast.31) | data formatting | bytes 4194304 | tf_op jit(solution)/shard_map/reshape | solution.py:172
  34.6 0.2 pad_maximum_fusion
  34.8 34.2 %all_to_all.16.q_ref = bf16[32,272,128]{2,1,0:T(8,128)(2,1)S(1)} all-to-all(bf16[32,272,128]{2,1,0:T(8,128)(2,1)S(1)} %pad_maximum_fusion), channel_id=1, replica_groups=mesh['y'=4,'core'=2,'z'=8,'x'=4] {'y','core','x'}, dimensions={0} | all-to-all | bytes 4456448 | tf_op jit(solution)/shard_map/all_to_all | solution.py:177
  69.0 0.1 fusion.6
  69.1 0.1 reshape.112
  69.2 0.9 reshape.106.lists_ref
  70.1 0.2 slice_reduce_fusion.counts_ref
  70.2 0.0 copy-start.4
  70.2 0.1 reshape_squeeze.3
  70.3 0.1 reduce_max.9
  70.5 0.7 reduce-window.9
  71.2 0.5 fusion.11.step_ref
  71.7 11.4 %all-gather.2.cloned.1.call-done.k_ref.v_ref = bf16[8192,256]{1,0:T(8,128)(2,1)} async-done(((bf16[1024,256]{1,0:T(8,128)(2,1)}), bf16[8192,256]{1,0:T(8,128)(2,1)}) %all-gather.2.cloned.1.call-update) | async-done | bytes 4194320 | tf_op jit(solution)/shard_map/all_gather | solution.py:161
  83.0 15.4 %shard_map.55 = (bf16[64,128,512]{2,1,0:T(8,128)(2,1)}, bf16[64,128,512]{2,1,0:T(8,128)(2,1)}) custom-call(s32[8]{0:T(128)} %fusion.11.step_ref, s32[8]{0:T(128)} %bitcast.33, s32[512]{0:T(512)} %reshape.106.lists_ref, s32[64]{0:T(128)} %copy-done.4, bf16[32,272,128]{2,1,0:T(8,128)(2,1)} %copy-done.1, bf16[8192,256]{1,0:T(8,128)(2,1)} %all-gather.2.cloned.1.call-done.k_ref.v_ref), custom_call_target="tpu_custom_call" | custom-call | flops 1073741824 | bytes 12582912 | tf_op jit(solution)/shard_map/pallas_call | solution.py:90
  98.4 12.0 %shard_map.56 = bf16[64,128,128]{2,1,0:T(8,128)(2,1)} custom-call(s32[8]{0:T(128)} %fusion.11.step_ref, s32[8]{0:T(128)} %bitcast.34, s32[512]{0:T(512)} %reshape.106.lists_ref, bf16[64,128,512]{2,1,0:T(8,128)(2,1)} %get-tuple-element.19.wlo_ref, bf16[64,128,512]{2,1,0:T(8,128)(2,1)} %get-tuple-element.20.whi_ref, ...), custom_call_target="tpu_custom_call" | custom-call | flops 1073741824 | bytes 12582912 | tf_op jit(solution)/shard_map/pallas_call | solution.py:114
  110.4 34.8 %all_to_all.17 = bf16[32,256,128]{2,1,0:T(8,128)(2,1)S(1)} all-to-all(bf16[32,256,128]{2,1,0:T(8,128)(2,1)} %bitcast.29), channel_id=1, replica_groups=mesh['y'=4,'core'=2,'z'=8,'x'=4] {'y','core','x'}, dimensions={0} | all-to-all | bytes 4194304 | tf_op jit(solution)/shard_map/all_to_all | solution.py:186
  145.2 1.6 %copy_bitcast_fusion = bf16[256,4096]{1,0:T(8,128)(2,1)} fusion(bf16[32,256,128]{2,1,0:T(8,128)(2,1)S(1)} %all_to_all.17), kind=kLoop, calls=%fused_computation.1 | loop fusion | bytes 4194304 | tf_op jit(solution)/shard_map/reshape | solution.py:189
  (11 shorter events, 0.1 us)
Async XLA Ops:
  6.5 1.0 copy-start
  6.5 22.0 %copy-start.5 = (s32[64]{0:T(128)S(1)}, s32[64]{0:T(128)}, u32[]{:S(2)}) copy-start(s32[64]{0:T(128)} %param.11) | copy-start | bytes 772
  6.5 22.1 %copy-start.3 = (s32[64,8]{0,1:T(8,128)S(1)}, s32[64,8]{0,1:T(8,128)}, u32[]{:S(2)}) copy-start(s32[64,8]{0,1:T(8,128)} %param.10) | copy-start | bytes 6148
  6.5 22.4 %copy-start.2 = (bf16[256,4096]{1,0:T(8,128)(2,1)S(1)}, bf16[256,4096]{1,0:T(8,128)(2,1)}, u32[]{:S(2)}) copy-start(bf16[256,4096]{1,0:T(8,128)(2,1)} %param.7) | copy-start | bytes 6291460
  6.5 76.5 %all-gather.2.cloned.1.call-start = ((), (), s32[]{:S(2)}) async-start(), calls=%async_computation.3 | async-start | bytes 4718592 | tf_op jit(solution)/shard_map/all_gather | solution.py:161
  69.0 14.0 %copy-start.1 = (bf16[32,272,128]{2,1,0:T(8,128)(2,1)}, bf16[32,272,128]{2,1,0:T(8,128)(2,1)S(1)}, u32[]{:S(2)}) copy-start(bf16[32,272,128]{2,1,0:T(8,128)(2,1)S(1)} %all_to_all.16.q_ref) | copy-start | bytes 6684676
  70.2 12.8 %copy-start.4 = (s32[64]{0:T(128)}, s32[64]{0:T(128)S(1)}, u32[]{:S(2)}) copy-start(s32[64]{0:T(128)S(1)} %slice_reduce_fusion.counts_ref) | copy-start | bytes 772
Sparse Core Ops, SparseCore 0:
  28.6 54.3 all-gather.1

commit v11 on v9

--- a/solution.py
+++ b/solution.py
@@ -66,7 +66,7 @@
 def attend(q_src, kv_rows, lists, counts, per_dev):
     sources = q_src.shape[0]
     blocks = sources * per_dev
-    per_src = 4 if sources % 4 == 0 else 1
+    per_src = 2 if sources % 2 == 0 else 1
     per_step = per_src * per_dev
     nk = kv_rows.shape[0]
     width = MOST * BLK

time: 152 us -> 161 us (1.059)
  Pallas kernels: 24.5 us -> 34.4 us
    pallas_call x1, Pallas kernels: 12.6 us -> 18 us  [attend(): pl.pallas_call(functools.partial(weights_kernel, per_step=per_step, per_d...]
    pallas_call x1, Pallas kernels: 11.9 us -> 16.4 us  [attend(): pl.pallas_call(functools.partial(mix_kernel, per_step=per_step), grid_spe...]
where the time goes in v11:
time: 161 us
  blocking collectives  88.9 us (55%)
  Pallas kernels  34.4 us (21%)
  between operations  13.5 us (8%)
  waiting for transfers between devices  12.1 us (8%)
  local copies, waits for them, and re-layouts  10.6 us (7%)
    all_to_all x1, blocking collectives, per_device(): lax.all_to_all(produced.reshape(group_count, rows, HD), group, split_axis...  34.8 us
    all_to_all x1, blocking collectives, per_device(): lax.all_to_all(q_heads, group, split_axis=0, concat_axis=0, tiled=True)  34.2 us
    all_to_all x1, blocking collectives, per_device(): lax.all_to_all(kv_heads, group, split_axis=0, concat_axis=0, tiled=True)  19.9 us
    pallas_call x1, Pallas kernels, attend(): pl.pallas_call(functools.partial(weights_kernel, per_step=per_step, per_d...  18 us
    pallas_call x1, Pallas kernels, attend(): pl.pallas_call(functools.partial(mix_kernel, per_step=per_step), grid_spe...  16.4 us
    all_gather x1, waiting for transfers between devices, per_device(): kv_rows = lax.all_gather(kv_part, 'z', axis=0, tiled=True)  12.1 us
    unnamed x13, local copies, waits for them, and re-layouts  3.36 us
  transfers between devices with their start and end apart: 1, of which 1 were waited for; matrix products, arithmetic and copies ran while one was open for 5% of the time, Pallas kernels for 0%

profile of v11, /device:TPU:1, one launch (start us, length us, event | category | flops | bytes accessed | tf_op | source)
XLA Modules:
  0.0 160.7 jit_solution(8202931630460490131)
XLA Ops:
  6.5 0.0 copy-start
  6.5 0.0 all-gather.2.cloned.1.call-start
  6.6 0.9 copy-done
  7.5 1.0 bitcast_bitcast_fusion
  8.5 0.1 pad_maximum_fusion.1
  8.6 19.9 %all_to_all.15 = bf16[32,32,256]{2,1,0:T(8,128)(2,1)} all-to-all(bf16[32,32,256]{2,1,0:T(8,128)(2,1)S(1)} %pad_maximum_fusion.1), channel_id=1, replica_groups=mesh['y'=4,'core'=2,'z'=8,'x'=4] {'y','core','x'}, dimensions={0} | all-to-all | bytes 1048576 | tf_op jit(solution)/shard_map/all_to_all | solution.py:143
  28.5 0.0 all-gather.2.cloned.1.call-update
  28.5 0.0 copy-done.5
  28.5 0.1 convert_bitcast_fusion
  28.6 0.0 copy-done.4
  28.6 0.1 dynamic-slice_convert_fusion
  28.7 0.1 copy.19
  28.8 0.1 convert_element_type.34
  28.9 0.0 copy-done.2
  28.9 2.4 %copy.17 = bf16[256,4096]{0,1:T(8,128)(2,1)} copy(bf16[256,4096]{1,0:T(8,128)(2,1)S(1)} %copy-done.2) | data formatting | bytes 4194304 | tf_op args[0]
  31.3 3.2 %copy.18 = bf16[256,32,128]{2,0,1:T(8,128)(2,1)S(1)} copy(bf16[256,32,128]{0,2,1:T(8,128)(2,1)} %bitcast.27) | data formatting | bytes 4194304 | tf_op jit(solution)/shard_map/reshape | solution.py:156
  34.6 0.2 pad_maximum_fusion
  34.8 34.2 %all_to_all.16.q_ref = bf16[32,272,128]{2,1,0:T(8,128)(2,1)S(1)} all-to-all(bf16[32,272,128]{2,1,0:T(8,128)(2,1)S(1)} %pad_maximum_fusion), channel_id=1, replica_groups=mesh['y'=4,'core'=2,'z'=8,'x'=4] {'y','core','x'}, dimensions={0} | all-to-all | bytes 4456448 | tf_op jit(solution)/shard_map/all_to_all | solution.py:161
  69.0 0.1 fusion.6
  69.1 0.1 reshape.75
  69.2 0.8 reshape.69.lists_ref
  70.0 0.2 slice_reduce_fusion.counts_ref
  70.2 0.0 copy-start.3
  70.2 0.1 reshape_squeeze.3
  70.3 0.1 reduce_max.9
  70.4 0.5 fusion.11.step_ref
  70.9 12.1 %all-gather.2.cloned.1.call-done.k_ref.v_ref = bf16[8192,256]{1,0:T(8,128)(2,1)} async-done(((bf16[1024,256]{1,0:T(8,128)(2,1)}), bf16[8192,256]{1,0:T(8,128)(2,1)}) %all-gather.2.cloned.1.call-update) | async-done | bytes 4194320 | tf_op jit(solution)/shard_map/all_gather | solution.py:145
  83.0 0.0 copy-done.1
  83.0 18.0 %shard_map.55.w_ref = bf16[64,128,1024]{2,1,0:T(8,128)(2,1)} custom-call(s32[16]{0:T(128)} %fusion.11.step_ref, s32[512]{0:T(512)} %reshape.69.lists_ref, s32[64]{0:T(128)} %copy-done.3, bf16[32,272,128]{2,1,0:T(8,128)(2,1)} %copy-done.1, bf16[8192,256]{1,0:T(8,128)(2,1)} %all-gather.2.cloned.1.call-done.k_ref.v_ref), custom_call_target="tpu_custom_call" | custom-call | flops 2147483648 | bytes 20971520 | tf_op jit(solution)/shard_map/pallas_call | solution.py:78
  101.1 16.4 %shard_map.56 = bf16[64,128,128]{2,1,0:T(8,128)(2,1)} custom-call(s32[16]{0:T(128)} %fusion.11.step_ref, s32[512]{0:T(512)} %reshape.69.lists_ref, bf16[64,128,1024]{2,1,0:T(8,128)(2,1)} %shard_map.55.w_ref, bf16[8192,256]{1,0:T(8,128)(2,1)} %all-gather.2.cloned.1.call-done.k_ref.v_ref), custom_call_target="tpu_custom_call" | custom-call | flops 2147483648 | bytes 20971520 | tf_op jit(solution)/shard_map/pallas_call | solution.py:99
  117.5 34.8 %all_to_all.17 = bf16[32,256,128]{2,1,0:T(8,128)(2,1)S(1)} all-to-all(bf16[32,256,128]{2,1,0:T(8,128)(2,1)} %bitcast.28), channel_id=1, replica_groups=mesh['y'=4,'core'=2,'z'=8,'x'=4] {'y','core','x'}, dimensions={0} | all-to-all | bytes 4194304 | tf_op jit(solution)/shard_map/all_to_all | solution.py:170
  152.3 1.6 %copy_bitcast_fusion = bf16[256,4096]{1,0:T(8,128)(2,1)} fusion(bf16[32,256,128]{2,1,0:T(8,128)(2,1)S(1)} %all_to_all.17), kind=kLoop, calls=%fused_computation.1 | loop fusion | bytes 4194304 | tf_op jit(solution)/shard_map/reshape | solution.py:173
  (9 shorter events, 0.1 us)
Async XLA Ops:
  6.5 1.0 copy-start
  6.5 22.0 %copy-start.5 = (s32[64]{0:T(128)S(1)}, s32[64]{0:T(128)}, u32[]{:S(2)}) copy-start(s32[64]{0:T(128)} %param.11) | copy-start | bytes 772
  6.5 22.1 %copy-start.4 = (s32[64,8]{0,1:T(8,128)S(1)}, s32[64,8]{0,1:T(8,128)}, u32[]{:S(2)}) copy-start(s32[64,8]{0,1:T(8,128)} %param.10) | copy-start | bytes 6148
  6.5 22.4 %copy-start.2 = (bf16[256,4096]{1,0:T(8,128)(2,1)S(1)}, bf16[256,4096]{1,0:T(8,128)(2,1)}, u32[]{:S(2)}) copy-start(bf16[256,4096]{1,0:T(8,128)(2,1)} %param.7) | copy-start | bytes 6291460
  6.5 76.5 %all-gather.2.cloned.1.call-start = ((), (), s32[]{:S(2)}) async-start(), calls=%async_computation.3 | async-start | bytes 4718592 | tf_op jit(solution)/shard_map/all_gather | solution.py:145
  69.0 14.0 %copy-start.1 = (bf16[32,272,128]{2,1,0:T(8,128)(2,1)}, bf16[32,272,128]{2,1,0:T(8,128)(2,1)S(1)}, u32[]{:S(2)}) copy-start(bf16[32,272,128]{2,1,0:T(8,128)(2,1)S(1)} %all_to_all.16.q_ref) | copy-start | bytes 6684676
  70.2 12.9 %copy-start.3 = (s32[64]{0:T(128)}, s32[64]{0:T(128)S(1)}, u32[]{:S(2)}) copy-start(s32[64]{0:T(128)S(1)} %slice_reduce_fusion.counts_ref) | copy-start | bytes 772
Sparse Core Ops, SparseCore 0:
  28.6 54.3 all-gather.1

commit v12 on v11

--- a/solution.py
+++ b/solution.py
@@ -66,7 +66,7 @@
 def attend(q_src, kv_rows, lists, counts, per_dev):
     sources = q_src.shape[0]
     blocks = sources * per_dev
-    per_src = 2 if sources % 2 == 0 else 1
+    per_src = 8 if sources % 8 == 0 else 1
     per_step = per_src * per_dev
     nk = kv_rows.shape[0]
     width = MOST * BLK

time: 161 us -> 153 us (0.950)
  Pallas kernels: 34.4 us -> 25.6 us
    pallas_call x1, Pallas kernels: 16.4 us -> 10.8 us  [attend(): pl.pallas_call(functools.partial(mix_kernel, per_step=per_step), grid_spe...]
    pallas_call x1, Pallas kernels: 18 us -> 14.8 us  [attend(): pl.pallas_call(functools.partial(weights_kernel, per_step=per_step, per_d...]
where the time goes in v12:
time: 153 us; the launch traced here: 152 us
  blocking collectives  88.9 us (58%)
  Pallas kernels  25.6 us (17%)
  between operations  13.5 us (9%)
  waiting for transfers between devices  12.1 us (8%)
  local copies, waits for them, and re-layouts  10.6 us (7%)
    all_to_all x1, blocking collectives, per_device(): lax.all_to_all(produced.reshape(group_count, rows, HD), group, split_axis...  34.8 us
    all_to_all x1, blocking collectives, per_device(): lax.all_to_all(q_heads, group, split_axis=0, concat_axis=0, tiled=True)  34.2 us
    all_to_all x1, blocking collectives, per_device(): lax.all_to_all(kv_heads, group, split_axis=0, concat_axis=0, tiled=True)  19.9 us
    pallas_call x1, Pallas kernels, attend(): pl.pallas_call(functools.partial(weights_kernel, per_step=per_step, per_d...  14.8 us
    all_gather x1, waiting for transfers between devices, per_device(): kv_rows = lax.all_gather(kv_part, 'z', axis=0, tiled=True)  12.1 us
    pallas_call x1, Pallas kernels, attend(): pl.pallas_call(functools.partial(mix_kernel, per_step=per_step), grid_spe...  10.8 us
    unnamed x13, local copies, waits for them, and re-layouts  3.36 us
    reshape x1, local copies, waits for them, and re-layouts, per_device(): queries.reshape(rows, HEADS, HD).transpose(1, 0, 2)  3.21 us
  transfers between devices with their start and end apart: 1, of which 1 were waited for; matrix products, arithmetic and copies ran while one was open for 5% of the time, Pallas kernels for 0%

profile of v12, /device:TPU:1, one launch (start us, length us, event | category | flops | bytes accessed | tf_op | source)
XLA Modules:
  0.0 151.9 jit_solution(12735964084163016436)
XLA Ops:
  6.5 0.0 copy-start
  6.5 0.0 all-gather.2.cloned.1.call-start
  6.6 0.9 copy-done
  7.5 1.0 bitcast_bitcast_fusion
  8.5 0.1 pad_maximum_fusion.1
  8.6 19.9 %all_to_all.15 = bf16[32,32,256]{2,1,0:T(8,128)(2,1)} all-to-all(bf16[32,32,256]{2,1,0:T(8,128)(2,1)S(1)} %pad_maximum_fusion.1), channel_id=1, replica_groups=mesh['y'=4,'core'=2,'z'=8,'x'=4] {'y','core','x'}, dimensions={0} | all-to-all | bytes 1048576 | tf_op jit(solution)/shard_map/all_to_all | solution.py:143
  28.5 0.0 all-gather.2.cloned.1.call-update
  28.5 0.0 copy-done.5
  28.5 0.1 convert_bitcast_fusion
  28.6 0.0 copy-done.4
  28.6 0.1 dynamic-slice_convert_fusion
  28.7 0.1 copy.19
  28.8 0.1 convert_element_type.34
  28.9 0.0 copy-done.2
  28.9 2.4 %copy.17 = bf16[256,4096]{0,1:T(8,128)(2,1)} copy(bf16[256,4096]{1,0:T(8,128)(2,1)S(1)} %copy-done.2) | data formatting | bytes 4194304 | tf_op args[0]
  31.3 3.2 %copy.18 = bf16[256,32,128]{2,0,1:T(8,128)(2,1)S(1)} copy(bf16[256,32,128]{0,2,1:T(8,128)(2,1)} %bitcast.27) | data formatting | bytes 4194304 | tf_op jit(solution)/shard_map/reshape | solution.py:156
  34.6 0.2 pad_maximum_fusion
  34.8 34.2 %all_to_all.16.q_ref = bf16[32,272,128]{2,1,0:T(8,128)(2,1)S(1)} all-to-all(bf16[32,272,128]{2,1,0:T(8,128)(2,1)S(1)} %pad_maximum_fusion), channel_id=1, replica_groups=mesh['y'=4,'core'=2,'z'=8,'x'=4] {'y','core','x'}, dimensions={0} | all-to-all | bytes 4456448 | tf_op jit(solution)/shard_map/all_to_all | solution.py:161
  69.0 0.1 fusion.6
  69.1 0.1 reshape.75
  69.2 0.8 reshape.69.lists_ref
  70.0 0.2 slice_reduce_fusion.counts_ref
  70.2 0.0 copy-start.3
  70.2 0.1 reshape_squeeze.3
  70.3 0.1 reduce_max.9
  70.4 0.5 fusion.11.step_ref
  70.9 12.1 %all-gather.2.cloned.1.call-done.k_ref.v_ref = bf16[8192,256]{1,0:T(8,128)(2,1)} async-done(((bf16[1024,256]{1,0:T(8,128)(2,1)}), bf16[8192,256]{1,0:T(8,128)(2,1)}) %all-gather.2.cloned.1.call-update) | async-done | bytes 4194320 | tf_op jit(solution)/shard_map/all_gather | solution.py:145
  83.0 0.0 copy-done.1
  83.0 14.8 %shard_map.55.w_ref = bf16[64,128,1024]{2,1,0:T(8,128)(2,1)} custom-call(s32[4]{0:T(128)} %fusion.11.step_ref, s32[512]{0:T(512)} %reshape.69.lists_ref, s32[64]{0:T(128)} %copy-done.3, bf16[32,272,128]{2,1,0:T(8,128)(2,1)} %copy-done.1, bf16[8192,256]{1,0:T(8,128)(2,1)} %all-gather.2.cloned.1.call-done.k_ref.v_ref), custom_call_target="tpu_custom_call" | custom-call | flops 2147483648 | bytes 20971520 | tf_op jit(solution)/shard_map/pallas_call | solution.py:78
  97.8 10.8 %shard_map.56 = bf16[64,128,128]{2,1,0:T(8,128)(2,1)} custom-call(s32[4]{0:T(128)} %fusion.11.step_ref, s32[512]{0:T(512)} %reshape.69.lists_ref, bf16[64,128,1024]{2,1,0:T(8,128)(2,1)} %shard_map.55.w_ref, bf16[8192,256]{1,0:T(8,128)(2,1)} %all-gather.2.cloned.1.call-done.k_ref.v_ref), custom_call_target="tpu_custom_call" | custom-call | flops 2147483648 | bytes 20971520 | tf_op jit(solution)/shard_map/pallas_call | solution.py:99
  108.6 34.8 %all_to_all.17 = bf16[32,256,128]{2,1,0:T(8,128)(2,1)S(1)} all-to-all(bf16[32,256,128]{2,1,0:T(8,128)(2,1)} %bitcast.28), channel_id=1, replica_groups=mesh['y'=4,'core'=2,'z'=8,'x'=4] {'y','core','x'}, dimensions={0} | all-to-all | bytes 4194304 | tf_op jit(solution)/shard_map/all_to_all | solution.py:170
  143.4 1.6 %copy_bitcast_fusion = bf16[256,4096]{1,0:T(8,128)(2,1)} fusion(bf16[32,256,128]{2,1,0:T(8,128)(2,1)S(1)} %all_to_all.17), kind=kLoop, calls=%fused_computation.1 | loop fusion | bytes 4194304 | tf_op jit(solution)/shard_map/reshape | solution.py:173
  (9 shorter events, 0.1 us)
Async XLA Ops:
  6.5 1.0 copy-start
  6.5 22.0 %copy-start.5 = (s32[64]{0:T(128)S(1)}, s32[64]{0:T(128)}, u32[]{:S(2)}) copy-start(s32[64]{0:T(128)} %param.11) | copy-start | bytes 772
  6.5 22.1 %copy-start.4 = (s32[64,8]{0,1:T(8,128)S(1)}, s32[64,8]{0,1:T(8,128)}, u32[]{:S(2)}) copy-start(s32[64,8]{0,1:T(8,128)} %param.10) | copy-start | bytes 6148
  6.5 22.4 %copy-start.2 = (bf16[256,4096]{1,0:T(8,128)(2,1)S(1)}, bf16[256,4096]{1,0:T(8,128)(2,1)}, u32[]{:S(2)}) copy-start(bf16[256,4096]{1,0:T(8,128)(2,1)} %param.7) | copy-start | bytes 6291460
  6.5 76.5 %all-gather.2.cloned.1.call-start = ((), (), s32[]{:S(2)}) async-start(), calls=%async_computation.3 | async-start | bytes 4718592 | tf_op jit(solution)/shard_map/all_gather | solution.py:145
  69.0 14.0 %copy-start.1 = (bf16[32,272,128]{2,1,0:T(8,128)(2,1)}, bf16[32,272,128]{2,1,0:T(8,128)(2,1)S(1)}, u32[]{:S(2)}) copy-start(bf16[32,272,128]{2,1,0:T(8,128)(2,1)S(1)} %all_to_all.16.q_ref) | copy-start | bytes 6684676
  70.2 12.9 %copy-start.3 = (s32[64]{0:T(128)}, s32[64]{0:T(128)S(1)}, u32[]{:S(2)}) copy-start(s32[64]{0:T(128)S(1)} %slice_reduce_fusion.counts_ref) | copy-start | bytes 772
Sparse Core Ops, SparseCore 0:
  28.6 54.3 all-gather.1

commit v13 on v9

--- a/solution.py
+++ b/solution.py
@@ -68,7 +68,7 @@
     blocks = sources * per_dev
     per_src = 4 if sources % 4 == 0 else 1
     per_step = per_src * per_dev
-    nk = kv_rows.shape[0]
+    nk = kv_rows.shape[1]
     width = MOST * BLK
     widest = jnp.max(counts.reshape(blocks // per_step, per_step), axis=1)
     step_size = jnp.zeros_like(widest)
@@ -83,7 +83,7 @@
             grid=(blocks // per_step,),
             in_specs=[
                 pl.BlockSpec((per_src, per_dev * BLK, HD), lambda b, *_: (b, 0, 0)),
-                pl.BlockSpec((nk, HD), lambda b, *_: (0, 0)),
+                pl.BlockSpec((None, nk, HD), lambda b, *_: (0, 0, 0)),
             ],
             out_specs=pl.BlockSpec((per_step, BLK, width), lambda b, *_: (b, 0, 0)),
             scratch_shapes=[pltpu.VMEM((width, HD), jnp.bfloat16)],
@@ -103,7 +103,7 @@
             grid=(blocks // per_step,),
             in_specs=[
                 pl.BlockSpec((per_step, BLK, width), lambda b, *_: (b, 0, 0)),
-                pl.BlockSpec((nk, HD), lambda b, *_: (0, 1)),
+                pl.BlockSpec((None, nk, HD), lambda b, *_: (1, 0, 0)),
             ],
             out_specs=pl.BlockSpec((per_step, BLK, HD), lambda b, *_: (b, 0, 0)),
             scratch_shapes=[pltpu.VMEM((width, HD), jnp.bfloat16)],
@@ -142,7 +142,8 @@
     )
     kv_split = lax.all_to_all(kv_heads, group, split_axis=0, concat_axis=0, tiled=True)
     kv_part = kv_split.reshape(group_count * tokens, 2 * HD)
-    kv_rows = lax.all_gather(kv_part, "z", axis=0, tiled=True)
+    kv_planes = kv_part.reshape(group_count * tokens, 2, HD).transpose(1, 0, 2)
+    kv_rows = lax.all_gather(kv_planes, "z", axis=1, tiled=True)
 
     kv_index = lax.axis_index("z") * x_count + lax.axis_index("x")
     own_lists = lax.dynamic_slice_in_dim(key_lists, kv_index * per_dev, per_dev, axis=0)

time: 152 us -> 155 us (1.020)
  Pallas kernels: 24.5 us -> 26.9 us
    pallas_call x1, Pallas kernels: 12.6 us -> 14.3 us  [attend(): pl.pallas_call(functools.partial(weights_kernel, per_step=per_step, per_d...]
where the time goes in v13:
time: 155 us; the launch traced here: 154 us
  blocking collectives  88.9 us (57%)
  Pallas kernels  26.9 us (17%)
  between operations  13.5 us (9%)
  waiting for transfers between devices  12.1 us (8%)
  local copies, waits for them, and re-layouts  11.6 us (7%)
    all_to_all x1, blocking collectives, per_device(): lax.all_to_all(produced.reshape(group_count, rows, HD), group, split_axis...  34.8 us
    all_to_all x1, blocking collectives, per_device(): lax.all_to_all(q_heads, group, split_axis=0, concat_axis=0, tiled=True)  34.2 us
    all_to_all x1, blocking collectives, per_device(): lax.all_to_all(kv_heads, group, split_axis=0, concat_axis=0, tiled=True)  19.9 us
    pallas_call x1, Pallas kernels, attend(): pl.pallas_call(functools.partial(weights_kernel, per_step=per_step, per_d...  14.3 us
    pallas_call x1, Pallas kernels, attend(): pl.pallas_call(functools.partial(mix_kernel, per_step=per_step), grid_spe...  12.6 us
    all_gather x1, waiting for transfers between devices, per_device(): kv_rows = lax.all_gather(kv_planes, 'z', axis=1, tiled=True)  12.1 us
    unnamed x13, local copies, waits for them, and re-layouts  3.41 us
    reshape x1, local copies, waits for them, and re-layouts, per_device(): queries.reshape(rows, HEADS, HD).transpose(1, 0, 2)  3.21 us
  transfers between devices with their start and end apart: 1, of which 1 were waited for; matrix products, arithmetic and copies ran while one was open for 5% of the time, Pallas kernels for 0%

profile of v13, /device:TPU:1, one launch (start us, length us, event | category | flops | bytes accessed | tf_op | source)
XLA Modules:
  0.0 154.2 jit_solution(6198186586527898692)
XLA Ops:
  6.5 0.9 copy-done
  7.5 1.0 bitcast_bitcast_fusion
  8.5 0.0 copy-start.5
  8.5 0.0 copy-start.4
  8.6 0.0 copy-start.2
  8.6 0.1 pad_maximum_fusion.1
  8.6 19.9 %all_to_all.15 = bf16[32,32,256]{2,1,0:T(8,128)(2,1)S(1)} all-to-all(bf16[32,32,256]{2,1,0:T(8,128)(2,1)S(1)} %pad_maximum_fusion.1), channel_id=1, replica_groups=mesh['y'=4,'core'=2,'z'=8,'x'=4] {'y','core','x'}, dimensions={0} | all-to-all | bytes 1048576 | tf_op jit(solution)/shard_map/all_to_all | solution.py:143
  28.6 0.1 reshape_reshape.3
  28.7 0.8 copy.30
  29.5 0.0 all-gather.2.cloned.1.call-update
  29.6 0.1 convert_bitcast_fusion
  29.6 0.0 copy-done.4
  29.7 0.1 dynamic-slice_convert_fusion
  29.7 0.1 copy.18
  29.8 0.1 convert_element_type.34
  29.9 2.4 %copy.16 = bf16[256,4096]{0,1:T(8,128)(2,1)} copy(bf16[256,4096]{1,0:T(8,128)(2,1)S(1)} %copy-done.2) | data formatting | bytes 4194304 | tf_op args[0]
  32.4 3.2 %copy.17 = bf16[256,32,128]{2,0,1:T(8,128)(2,1)S(1)} copy(bf16[256,32,128]{0,2,1:T(8,128)(2,1)} %bitcast.29) | data formatting | bytes 4194304 | tf_op jit(solution)/shard_map/reshape | solution.py:157
  35.6 0.2 pad_maximum_fusion
  35.8 34.2 %all_to_all.16.q_ref = bf16[32,272,128]{2,1,0:T(8,128)(2,1)S(1)} all-to-all(bf16[32,272,128]{2,1,0:T(8,128)(2,1)S(1)} %pad_maximum_fusion), channel_id=1, replica_groups=mesh['y'=4,'core'=2,'z'=8,'x'=4] {'y','core','x'}, dimensions={0} | all-to-all | bytes 4456448 | tf_op jit(solution)/shard_map/all_to_all | solution.py:162
  70.0 0.1 fusion.6
  70.1 0.1 reshape.71
  70.2 0.8 reshape.66.lists_ref
  71.0 0.2 slice_reduce_fusion.counts_ref
  71.2 0.0 copy-start.3
  71.2 0.1 reshape_squeeze.3
  71.3 0.1 reduce_max.9
  71.4 0.5 fusion.11.step_ref
  72.0 12.1 %all-gather.2.cloned.1.call-done.k_ref.v_ref = bf16[2,8192,128]{2,1,0:T(8,128)(2,1)} async-done(((bf16[2,1024,128]{2,1,0:T(8,128)(2,1)}), bf16[2,8192,128]{2,1,0:T(8,128)(2,1)}) %all-gather.2.cloned.1.call-update) | async-done | bytes 4194320 | tf_op jit(solution)/shard_map/all_gather | solution.py:146
  84.1 14.3 %shard_map.55.w_ref = bf16[64,128,1024]{2,1,0:T(8,128)(2,1)} custom-call(s32[8]{0:T(128)} %fusion.11.step_ref, s32[512]{0:T(512)} %reshape.66.lists_ref, s32[64]{0:T(128)} %copy-done.3, bf16[32,272,128]{2,1,0:T(8,128)(2,1)} %copy-done.1, bf16[2,8192,128]{2,1,0:T(8,128)(2,1)} %all-gather.2.cloned.1.call-done.k_ref.v_ref), custom_call_target="tpu_custom_call" | custom-call | flops 2147483648 | bytes 20971520 | tf_op jit(solution)/shard_map/pallas_call | solution.py:78
  98.4 12.6 %shard_map.56 = bf16[64,128,128]{2,1,0:T(8,128)(2,1)} custom-call(s32[8]{0:T(128)} %fusion.11.step_ref, s32[512]{0:T(512)} %reshape.66.lists_ref, bf16[64,128,1024]{2,1,0:T(8,128)(2,1)} %shard_map.55.w_ref, bf16[2,8192,128]{2,1,0:T(8,128)(2,1)} %all-gather.2.cloned.1.call-done.k_ref.v_ref), custom_call_target="tpu_custom_call" | custom-call | flops 2147483648 | bytes 20971520 | tf_op jit(solution)/shard_map/pallas_call | solution.py:99
  111.0 34.8 %all_to_all.17 = bf16[32,256,128]{2,1,0:T(8,128)(2,1)S(1)} all-to-all(bf16[32,256,128]{2,1,0:T(8,128)(2,1)} %bitcast.30), channel_id=1, replica_groups=mesh['y'=4,'core'=2,'z'=8,'x'=4] {'y','core','x'}, dimensions={0} | all-to-all | bytes 4194304 | tf_op jit(solution)/shard_map/all_to_all | solution.py:171
  145.8 1.6 %copy_bitcast_fusion = bf16[256,4096]{1,0:T(8,128)(2,1)} fusion(bf16[32,256,128]{2,1,0:T(8,128)(2,1)S(1)} %all_to_all.17), kind=kLoop, calls=%fused_computation.1 | loop fusion | bytes 4194304 | tf_op jit(solution)/shard_map/reshape | solution.py:174
  (11 shorter events, 0.1 us)
Async XLA Ops:
  6.5 1.0 copy-start
  6.5 77.6 %all-gather.2.cloned.1.call-start = ((), (), s32[]{:S(2)}) async-start(), calls=%async_computation.3 | async-start | bytes 4718592 | tf_op jit(solution)/shard_map/all_gather | solution.py:146
  8.5 21.0 %copy-start.5 = (s32[64]{0:T(128)S(1)}, s32[64]{0:T(128)}, u32[]{:S(2)}) copy-start(s32[64]{0:T(128)} %param.11) | copy-start | bytes 772
  8.5 21.1 %copy-start.4 = (s32[64,8]{0,1:T(8,128)S(1)}, s32[64,8]{0,1:T(8,128)}, u32[]{:S(2)}) copy-start(s32[64,8]{0,1:T(8,128)} %param.10) | copy-start | bytes 6148
  8.6 21.4 %copy-start.2 = (bf16[256,4096]{1,0:T(8,128)(2,1)S(1)}, bf16[256,4096]{1,0:T(8,128)(2,1)}, u32[]{:S(2)}) copy-start(bf16[256,4096]{1,0:T(8,128)(2,1)} %param.7) | copy-start | bytes 6291460
  70.0 14.1 %copy-start.1 = (bf16[32,272,128]{2,1,0:T(8,128)(2,1)}, bf16[32,272,128]{2,1,0:T(8,128)(2,1)S(1)}, u32[]{:S(2)}) copy-start(bf16[32,272,128]{2,1,0:T(8,128)(2,1)S(1)} %all_to_all.16.q_ref) | copy-start | bytes 6684676
  71.2 12.9 %copy-start.3 = (s32[64]{0:T(128)}, s32[64]{0:T(128)S(1)}, u32[]{:S(2)}) copy-start(s32[64]{0:T(128)S(1)} %slice_reduce_fusion.counts_ref) | copy-start | bytes 772
Sparse Core Ops, SparseCore 0:
  29.7 54.3 all-gather.1
